TPU v7x, 512 devices: a whole 4x8x8 slice. The times are simulated.
512 devices in a mesh: dp: 4 (over x), seq: 16 (over z, core), head: 8 (over y).
Axes of the slice: x: 4, y: 8, z: 8, core: 2. Of those that a mesh axis runs over, the one named last changes fastest.
Arguments:
- doc_ids: int32 [16384], P(('dp', 'seq')), parts along dimension 0, may hold values from 0 to 7, never falling along the last dimension, each value on 1 to 2048 neighbouring positions
- light_q: bfloat16 [16384, 4096], P(('dp', 'seq'), 'head'), parts along dimension 0, may hold values from -0.59765625 to 0.59765625
- light_k: bfloat16 [16384, 4096], P(('dp', 'seq'), 'head'), parts along dimension 0, may hold values from -0.59765625 to 0.59765625
- light_v: bfloat16 [16384, 4096], P(('dp', 'seq'), 'head'), parts along dimension 0, may hold values from -6 to 6
- light_decay: float32 [32], P('head'), may hold values from 0 to 1
- light_grad_out: bfloat16 [16384, 4096], P(('dp', 'seq'), 'head'), parts along dimension 0, may hold values from -6 to 6
- soft_q: bfloat16 [16384, 4096], P(('dp', 'seq'), 'head'), parts along dimension 0, may hold values from -40 to 40
- soft_k: bfloat16 [16384, 4096], P(('dp', 'seq'), 'head'), parts along dimension 0, may hold values from -40 to 40
- soft_v: bfloat16 [16384, 4096], P(('dp', 'seq'), 'head'), parts along dimension 0, may hold values from -6 to 6
- soft_grad_out: bfloat16 [16384, 4096], P(('dp', 'seq'), 'head'), parts along dimension 0, may hold values from -6 to 6
Outputs:
- lightning_output: bfloat16 [16384, 4096], P(('dp', 'seq'), 'head'), parts along dimension 0
- lightning_query_gradient: bfloat16 [16384, 4096], P(('dp', 'seq'), 'head'), parts along dimension 0
- lightning_key_gradient: bfloat16 [16384, 4096], P(('dp', 'seq'), 'head'), parts along dimension 0
- lightning_value_gradient: bfloat16 [16384, 4096], P(('dp', 'seq'), 'head'), parts along dimension 0
- soft_out: bfloat16 [16384, 4096], P(('dp', 'seq'), 'head'), parts along dimension 0
- soft_dq: bfloat16 [16384, 4096], P(('dp', 'seq'), 'head'), parts along dimension 0
- soft_dk: bfloat16 [16384, 4096], P(('dp', 'seq'), 'head'), parts along dimension 0
- soft_dv: bfloat16 [16384, 4096], P(('dp', 'seq'), 'head'), parts along dimension 0
There are 4 independent parts, one for each index of `dp`. A program takes and returns all parts, laid end to end along the dimension named above; an argument that names none is the same for every part. Nothing has to cross between parts.
Inputs may be any that keep to these rules, and one draw needn't show every extreme that they name: `doc_ids`: document ids never fall along the sequence; each document holds at most 2048 tokens, and one holds exactly that many.
All inputs are finite; a program needn't handle non-finite values.
Results may differ from a plain program's by a relative error of at most 0.02.
Values may be sent and summed in bfloat16 or wider, within the bound.
No kernel may reach another device: no remote copies, remote signals or barrier semaphores. Data moves between devices by JAX's collectives and lax.ppermute only.
A program may use at most 128 MiB of HBM per device.

v0:
```python
import jax
import jax.numpy as jnp
from jax import lax
from jax.sharding import PartitionSpec as P

PRECISE = lax.Precision.HIGH


def entering(part, axis, combine, identity, reverse):
    count = lax.axis_size(axis)
    place = lax.axis_index(axis)
    ahead = count - 1 - place if reverse else place
    gathered = jax.tree.map(lambda a: lax.all_gather(a, axis), part)
    state = jax.tree.map(lambda a, e: jnp.zeros_like(a) + jnp.asarray(e, a.dtype), part, identity)

    def one(lap, state):
        source = count - 1 - lap if reverse else lap
        return combine(
            state, jax.tree.map(lambda a: lax.dynamic_index_in_dim(a, source, 0, False), gathered)
        )

    return lax.fori_loop(0, ahead, one, state)


def from_behind(value, axis, steps):
    count = lax.axis_size(axis)
    first, last = (max(0, -steps), min(count, count - steps))
    return lax.ppermute(value, axis, [(source, source + steps) for source in range(first, last)])


def join_forward(earlier, later):
    state_a, keep_a, head_a, tail_a = earlier
    state_b, keep_b, head_b, tail_b = later
    empty_a = tail_a < 0
    empty_b = tail_b < 0
    joined = (head_b == tail_b) & (head_b == tail_a)
    running_state = jnp.where(
        empty_b, state_a, jnp.where(joined, keep_b[:, None, None] * state_a + state_b, state_b)
    )
    return (
        running_state,
        keep_a * keep_b,
        jnp.where(empty_a, head_b, head_a),
        jnp.where(empty_b, tail_a, tail_b),
    )


def join_backward(earlier, later):
    state_h, keep_h, head_h, tail_h = earlier
    state_l, keep_l, head_l, tail_l = later
    empty_h = tail_h < 0
    empty_l = tail_l < 0
    joined = (head_l == tail_l) & (tail_l == head_h)
    running_state = jnp.where(
        empty_l, state_h, jnp.where(joined, keep_l[:, None, None] * state_h + state_l, state_l)
    )
    return (
        running_state,
        keep_h * keep_l,
        jnp.where(empty_l, head_h, head_l),
        jnp.where(empty_h, tail_l, tail_h),
    )


def mixed_result(form, left, right):
    return jnp.einsum(form, left, right, precision=PRECISE, preferred_element_type=jnp.float32)


def per_device(
    doc_ids,
    light_q,
    light_k,
    light_v,
    light_decay,
    light_grad_out,
    soft_q,
    soft_k,
    soft_v,
    soft_grad_out,
):
    tok_rows = light_q.shape[0]
    heads = light_decay.shape[0]
    width = light_q.shape[1] // heads
    shards = lax.axis_size("seq")
    total_rows = tok_rows * shards
    offset = lax.axis_index("seq") * tok_rows
    last_pos = offset + tok_rows - 1
    all_ids = lax.all_gather(doc_ids, "seq", axis=0, tiled=True)
    positions = offset + jnp.arange(tok_rows, dtype=jnp.int32)
    own_ids = doc_ids.astype(jnp.float32)
    within_segment_position = jnp.arange(tok_rows, dtype=jnp.int32)
    reach = min(shards - 1, (tok_rows + total_rows // 2 - 2) // tok_rows)
    query_half_rows = light_q.reshape(tok_rows, heads, width)
    key_half_rows = light_k.reshape(tok_rows, heads, width)
    value_half_rows = light_v.reshape(tok_rows, heads, width)
    backward_sequence_share = light_grad_out.reshape(tok_rows, heads, width)
    inside = (doc_ids[:, None] == doc_ids[None, :]) & (
        within_segment_position[None, :] <= within_segment_position[:, None]
    )
    distance = jnp.maximum(
        within_segment_position[:, None] - within_segment_position[None, :], 0
    ).astype(jnp.float32)
    weight = jnp.where(inside[None], jnp.exp(-light_decay[:, None, None] * distance[None]), 0.0)
    scores = (
        jnp.einsum(
            "thd,shd->hts", query_half_rows, key_half_rows, preferred_element_type=jnp.float32
        )
        * weight
    )
    lightning_output = mixed_result("hts,shd->thd", scores, value_half_rows)
    head_id = own_ids[0]
    tail_id = own_ids[-1]
    since_start = (within_segment_position + 1).astype(jnp.float32)
    until_end = (tok_rows - 1 - within_segment_position).astype(jnp.float32)
    start_decay = jnp.exp(-since_start[:, None] * light_decay[None, :])
    end_decay = jnp.exp(-until_end[:, None] * light_decay[None, :])
    offset_to_end = end_decay * (own_ids == tail_id)[:, None]
    running_state = mixed_result(
        "bto,btq->toq", key_half_rows * offset_to_end[:, :, None], value_half_rows
    )
    keep = jnp.exp(-light_decay * tok_rows)
    identity = (
        jnp.zeros_like(running_state),
        jnp.ones_like(keep),
        jnp.float32(-1.0),
        jnp.float32(-1.0),
    )
    inherited_memory_matrix, _, _, carried_id = entering(
        (running_state, keep, head_id, tail_id), "seq", join_forward, identity, False
    )
    distance_since_beginning = start_decay * (own_ids == carried_id)[:, None]
    lightning_output = lightning_output + mixed_result(
        "peb,ebi->pei",
        query_half_rows * distance_since_beginning[:, :, None],
        inherited_memory_matrix,
    )
    grad_scores = (
        jnp.einsum(
            "thv,shv->hts",
            backward_sequence_share,
            value_half_rows,
            preferred_element_type=jnp.float32,
        )
        * weight
    )
    lightning_query_gradient = mixed_result("hts,shk->thk", grad_scores, key_half_rows)
    lightning_query_gradient = lightning_query_gradient + mixed_result(
        "mcq,cxq->mcx",
        backward_sequence_share * distance_since_beginning[:, :, None],
        inherited_memory_matrix,
    )
    lightning_key_gradient = mixed_result("hts,thk->shk", grad_scores, query_half_rows)
    lightning_value_gradient = mixed_result("hts,thv->shv", scores, backward_sequence_share)
    opening_part = start_decay * (own_ids == head_id)[:, None]
    pending_state = mixed_result(
        "ejn,ejf->jnf", query_half_rows * opening_part[:, :, None], backward_sequence_share
    )
    returned_value, _, yielded_document_number, _ = entering(
        (pending_state, keep, head_id, tail_id), "seq", join_backward, identity, True
    )
    closing_part = (end_decay * (own_ids == yielded_document_number)[:, None])[:, :, None]
    lightning_key_gradient = (
        lightning_key_gradient
        + mixed_result("qpb,aqb->aqp", returned_value, value_half_rows) * closing_part
    )
    lightning_value_gradient = (
        lightning_value_gradient
        + mixed_result("dgp,zdg->zdp", returned_value, key_half_rows) * closing_part
    )
    scale = width ** (-0.5)
    soft_query = soft_q.reshape(tok_rows, heads, width)
    soft_grads = soft_grad_out.reshape(tok_rows, heads, width)
    soft_keys = soft_k.reshape(tok_rows, heads, width)
    soft_values = soft_v.reshape(tok_rows, heads, width)
    all_keys, all_values = (
        lax.all_gather(soft_k, "seq", axis=0, tiled=True),
        lax.all_gather(soft_v, "seq", axis=0, tiled=True),
    )
    first_pos = jnp.sum(all_ids < doc_ids[0])
    doc_end = jnp.sum(all_ids <= doc_ids[-1]) - 1
    key_block = min(512, total_rows)
    key_count = total_rows // key_block
    block_order = jnp.arange(key_count, dtype=jnp.int32)

    def key_mask(start, count):
        key_pos = start + jnp.arange(count, dtype=jnp.int32)
        key_ids = lax.dynamic_slice_in_dim(all_ids, start, count)
        return (key_pos[None, :] <= positions[:, None]) & (key_ids[None, :] == doc_ids[:, None])

    def held_block(start):
        segment_attention_inputs = lax.dynamic_slice_in_dim(all_keys, start, key_block).reshape(
            key_block, heads, width
        )
        block_values = lax.dynamic_slice_in_dim(all_values, start, key_block).reshape(
            key_block, heads, width
        )
        return (segment_attention_inputs, block_values)

    def unused(start):
        return (start > last_pos) | (start + key_block - 1 < first_pos)

    def forward_block(carry, index):
        start = index * key_block

        def forward_update(inner):
            top, total, accum = inner
            segment_attention_inputs, block_values = held_block(start)
            allowed = key_mask(start, key_block)[None]
            logits = (
                jnp.einsum(
                    "thd,shd->hts",
                    soft_query,
                    segment_attention_inputs,
                    preferred_element_type=jnp.float32,
                )
                * scale
            )
            logits = jnp.where(allowed, logits, -1e30)
            fresh = jnp.maximum(top, jnp.max(logits, axis=2))
            factor = jnp.exp(top - fresh)
            expo = jnp.where(allowed, jnp.exp(logits - fresh[:, :, None]), 0.0)
            total = total * factor + jnp.sum(expo, axis=2)
            accum = accum * factor[:, :, None] + jnp.einsum(
                "hts,shd->htd",
                expo.astype(jnp.bfloat16),
                block_values,
                preferred_element_type=jnp.float32,
            )
            return (fresh, total, accum)

        return (lax.cond(unused(start), lambda inner: inner, forward_update, carry), None)

    start_carry = (
        jnp.full((heads, tok_rows), -1e30, jnp.float32),
        jnp.zeros((heads, tok_rows), jnp.float32),
        jnp.zeros((heads, tok_rows, width), jnp.float32),
    )
    (top, total, accum), _ = lax.scan(forward_block, start_carry, block_order)
    soft_out = jnp.transpose(accum / total[:, :, None], (1, 0, 2)).astype(jnp.bfloat16)
    lse = top + jnp.log(total)
    delta = jnp.sum(soft_grads.astype(jnp.float32) * soft_out.astype(jnp.float32), axis=2).T
    all_lse, all_delta = (
        lax.all_gather(lse, "seq", axis=1, tiled=True),
        lax.all_gather(delta, "seq", axis=1, tiled=True),
    )
    zero_rows = jnp.zeros((tok_rows, heads, width), jnp.float32)

    def query_block(carry, index):
        start = index * key_block

        def query_update(inner):
            segment_attention_inputs, block_values = held_block(start)
            allowed = key_mask(start, key_block)[None]
            logits = (
                jnp.einsum(
                    "thd,shd->hts",
                    soft_query,
                    segment_attention_inputs,
                    preferred_element_type=jnp.float32,
                )
                * scale
            )
            prob = jnp.where(
                allowed, jnp.exp(jnp.where(allowed, logits - lse[:, :, None], -1e30)), 0.0
            )
            dprob = jnp.einsum(
                "thd,shd->hts", soft_grads, block_values, preferred_element_type=jnp.float32
            )
            dlogit = (prob * (dprob - delta[:, :, None])).astype(jnp.bfloat16)
            return (
                inner
                + jnp.einsum(
                    "hts,shd->thd",
                    dlogit,
                    segment_attention_inputs,
                    preferred_element_type=jnp.float32,
                )
                * scale
            )

        return (lax.cond(unused(start), lambda inner: inner, query_update, carry), None)

    soft_dq, _ = lax.scan(query_block, zero_rows, block_order)

    def key_terms(piece_query, piece_grads, start, count):
        query_pos = start + jnp.arange(count, dtype=jnp.int32)
        query_ids = lax.dynamic_slice_in_dim(all_ids, start, count)
        lse_part = lax.dynamic_slice_in_dim(all_lse, start, count, 1)
        delta_part = lax.dynamic_slice_in_dim(all_delta, start, count, 1)
        allowed = (
            (positions[None, :] <= query_pos[:, None]) & (doc_ids[None, :] == query_ids[:, None])
        )[None]
        logits = (
            jnp.einsum("thd,shd->hts", piece_query, soft_keys, preferred_element_type=jnp.float32)
            * scale
        )
        prob = jnp.where(
            allowed, jnp.exp(jnp.where(allowed, logits - lse_part[:, :, None], -1e30)), 0.0
        )
        dv_part = jnp.einsum(
            "hts,thd->shd",
            prob.astype(jnp.bfloat16),
            piece_grads,
            preferred_element_type=jnp.float32,
        )
        dprob = jnp.einsum(
            "thd,shd->hts", piece_grads, soft_values, preferred_element_type=jnp.float32
        )
        dlogit = (prob * (dprob - delta_part[:, :, None])).astype(jnp.bfloat16)
        dk_part = (
            jnp.einsum("hts,thd->shd", dlogit, piece_query, preferred_element_type=jnp.float32)
            * scale
        )
        return (dk_part, dv_part)

    def key_piece(carry, piece_query, piece_grads, start):
        count = piece_query.shape[0]
        span_rows = count
        span_count = count // span_rows

        def span_step(inner, index):
            begin = index * span_rows
            query_part = piece_query.reshape(span_rows, heads, width)
            grads_part = piece_grads.reshape(span_rows, heads, width)
            query_start = start + begin

            def span_update(sums):
                dk_part, dv_part = key_terms(query_part, grads_part, query_start, span_rows)
                return (sums[0] + dk_part, sums[1] + dv_part)

            skipped = (query_start + span_rows - 1 < offset) | (query_start > doc_end)
            return (lax.cond(skipped, lambda sums: sums, span_update, inner), None)

        result, _ = lax.scan(span_step, carry, jnp.arange(span_count, dtype=jnp.int32))
        return result

    grad_pair = key_piece((zero_rows, zero_rows), soft_q, soft_grad_out, offset)
    for step in range(1, reach + 1):
        near_query, near_grads = from_behind((soft_q, soft_grad_out), "seq", -step)
        later_start = jnp.minimum(offset + step * tok_rows, total_rows - tok_rows)
        grad_pair = key_piece(grad_pair, near_query, near_grads, later_start)
    soft_dk, soft_dv = grad_pair
    flat = (tok_rows, heads * width)
    return (
        lightning_output.reshape(flat).astype(jnp.bfloat16),
        lightning_query_gradient.reshape(flat).astype(jnp.bfloat16),
        lightning_key_gradient.reshape(flat).astype(jnp.bfloat16),
        lightning_value_gradient.reshape(flat).astype(jnp.bfloat16),
        soft_out.reshape(flat),
        soft_dq.reshape(flat).astype(jnp.bfloat16),
        soft_dk.reshape(flat).astype(jnp.bfloat16),
        soft_dv.reshape(flat).astype(jnp.bfloat16),
    )


def solution(mesh):
    return jax.shard_map(
        per_device,
        mesh=mesh,
        in_specs=(
            P(("dp", "seq")),
            P(("dp", "seq"), "head"),
            P(("dp", "seq"), "head"),
            P(("dp", "seq"), "head"),
            P("head"),
            P(("dp", "seq"), "head"),
            P(("dp", "seq"), "head"),
            P(("dp", "seq"), "head"),
            P(("dp", "seq"), "head"),
            P(("dp", "seq"), "head"),
        ),
        out_specs=(
            P(("dp", "seq"), "head"),
            P(("dp", "seq"), "head"),
            P(("dp", "seq"), "head"),
            P(("dp", "seq"), "head"),
            P(("dp", "seq"), "head"),
            P(("dp", "seq"), "head"),
            P(("dp", "seq"), "head"),
            P(("dp", "seq"), "head"),
        ),
        check_vma=False,
    )
```

profile of v0, /device:TPU:455, one launch (start us, length us, event | category | flops | bytes accessed | tf_op | source)
XLA Modules:
  0.0 607.9 jit_solution(9035415345638498831)
XLA Ops:
  19.4 24.3 %all-reduce.3 = (f32[16]{0:T(128)S(1)}, f32[16]{0:T(128)S(1)}, f32[64]{0:T(128)S(1)}) all-reduce(f32[16]{0:T(128)S(1)} %get-tuple-element.2322, f32[16]{0:T(128)S(1)} %slice_dynamic-update-slice_fusion, f32[64]{0:T(128)S(1)} %get-tuple-element.2325), channel_id=1, replica_groups=mesh['dp'=4,'seq'=16,'head'=8] {'seq'}, use_global_device_ids=true, to_apply=%add | all-reduce | flops 96 | bytes 768
  44.0 15.3 %all-gather.15.cloned.1.call-done = f32[64,128,128]{2,1,0:T(8,128)} async-done(((f32[4,128,128]{2,1,0:T(8,128)}), f32[64,128,128]{2,1,0:T(8,128)}) %all-gather.15.cloned.1.call-update) | async-done | bytes 4194320 | tf_op jit(solution)/shard_map/all_gather | solution.py:13
  62.6 8.3 %collective-permute-start.15 = (bf16[256,512]{0,1:T(8,128)(2,1)}, bf16[256,512]{0,1:T(8,128)(2,1)}, u32[]{:S(2)}, u32[]{:S(2)}) collective-permute-start(bf16[256,512]{0,1:T(8,128)(2,1)} %copy.333), channel_id=1, source_target_pairs={{8,0},{16,8},{24,16},{32,24},{40,32},{48,40},{56,48},{64,56},{72,6... | collective-permute-start | bytes 786440 | tf_op jit(solution)/shard_map/ppermute | solution.py:28
  70.9 13.3 %collective-permute-start.13 = (bf16[256,512]{0,1:T(8,128)(2,1)}, bf16[256,512]{0,1:T(8,128)(2,1)}, u32[]{:S(2)}, u32[]{:S(2)}) collective-permute-start(bf16[256,512]{0,1:T(8,128)(2,1)} %copy.333), channel_id=1, source_target_pairs={{16,0},{24,8},{32,16},{40,24},{48,32},{56,40},{64,48},{72,56},{80,... | collective-permute-start | bytes 786440 | tf_op jit(solution)/shard_map/ppermute | solution.py:28
  85.0 9.0 %collective-permute-start.14 = (bf16[256,512]{0,1:T(8,128)(2,1)}, bf16[256,512]{0,1:T(8,128)(2,1)}, u32[]{:S(2)}, u32[]{:S(2)}) collective-permute-start(bf16[256,512]{0,1:T(8,128)(2,1)} %copy.329), channel_id=1, source_target_pairs={{8,0},{16,8},{24,16},{32,24},{40,32},{48,40},{56,48},{64,56},{72,6... | collective-permute-start | bytes 786440 | tf_op jit(solution)/shard_map/ppermute | solution.py:28
  94.0 13.3 %collective-permute-start.12 = (bf16[256,512]{0,1:T(8,128)(2,1)}, bf16[256,512]{0,1:T(8,128)(2,1)}, u32[]{:S(2)}, u32[]{:S(2)}) collective-permute-start(bf16[256,512]{0,1:T(8,128)(2,1)} %copy.329), channel_id=1, source_target_pairs={{16,0},{24,8},{32,16},{40,24},{48,32},{56,40},{64,48},{72,56},{80,... | collective-permute-start | bytes 786440 | tf_op jit(solution)/shard_map/ppermute | solution.py:28
  107.3 19.6 %collective-permute-start.11 = (bf16[256,512]{0,1:T(8,128)(2,1)}, bf16[256,512]{0,1:T(8,128)(2,1)S(1)}, u32[]{:S(2)}, u32[]{:S(2)}) collective-permute-start(bf16[256,512]{0,1:T(8,128)(2,1)} %copy.333), channel_id=1, source_target_pairs={{24,0},{32,8},{40,16},{48,24},{56,32},{64,40},{72,48},{80,56},{88,... | collective-permute-start | bytes 786440 | tf_op jit(solution)/shard_map/ppermute | solution.py:28
  127.0 62.3 %all-gather.3 = s32[16,1,256]{2,1,0:T(1,128)} all-gather(s32[1,1,256]{2,1,0:T(1,128)S(1)} %bitcast.397), channel_id=1, replica_groups=mesh['dp'=4,'seq'=16,'head'=8] {'seq'}, dimensions={0}, use_global_device_ids=true | all-gather | bytes 17408 | tf_op jit(solution)/shard_map/all_gather | solution.py:88
  198.4 25.5 %while.47 = (s32[]{:T(128)}, f32[4,256]{1,0:T(4,128)S(1)}, f32[4,256]{1,0:T(4,128)S(1)}, f32[4,256,128]{2,1,0:T(8,128)S(1)}, s32[8]{0:T(128)S(1)}, /*index=5*/s3...) while((s32[]{:T(128)}, f32[4,256]{1,0:T(4,128)S(1)}, ...), condition=%wide.region_10.11_spmd.clone, body=%wide.region_5.10_spmd.clone.sunk | while | flops 275909376 | bytes 11353485 | solution.py:238
  230.0 17.0 %collective-permute-start.9 = (bf16[256,512]{0,1:T(8,128)(2,1)}, bf16[256,512]{0,1:T(8,128)(2,1)}, u32[]{:S(2)}, u32[]{:S(2)}) collective-permute-start(bf16[256,512]{0,1:T(8,128)(2,1)} %copy.333), channel_id=1, source_target_pairs={{32,0},{40,8},{48,16},{56,24},{64,32},{72,40},{80,48},{88,56},{96,... | collective-permute-start | bytes 786440 | tf_op jit(solution)/shard_map/ppermute | solution.py:28
  253.1 29.9 %collective-permute-start.5 = (bf16[256,512]{0,1:T(8,128)(2,1)}, bf16[256,512]{0,1:T(8,128)(2,1)}, u32[]{:S(2)}, u32[]{:S(2)}) collective-permute-start(bf16[256,512]{0,1:T(8,128)(2,1)} %copy.333), channel_id=1, source_target_pairs={{48,0},{56,8},{64,16},{72,24},{80,32},{88,40},{96,48},{104,56},{11... | collective-permute-start | bytes 786440 | tf_op jit(solution)/shard_map/ppermute | solution.py:28
  284.4 35.8 %while.48 = (s32[]{:T(128)}, f32[256,4,128]{0,2,1:T(8,128)}, s32[8]{0:T(128)}, s32[]{:T(128)}, s32[]{:T(128)}, /*index=5*/bf16[4096,512]{0,1:T(8,128)(2,1)}, s32...) while((s32[]{:T(128)}, f32[256,4,128]{0,2,1:T(8,128)}, ...), condition=%wide.region_15.16_spmd.clone, body=%wide.region_12.15_spmd.clone.sunk | while | flops 406979328 | bytes 9739665 | solution.py:283
  325.4 16.8 %collective-permute-start.4 = (bf16[256,512]{0,1:T(8,128)(2,1)}, bf16[256,512]{0,1:T(8,128)(2,1)}, u32[]{:S(2)}, u32[]{:S(2)}) collective-permute-start(bf16[256,512]{0,1:T(8,128)(2,1)} %copy.329), channel_id=1, source_target_pairs={{48,0},{56,8},{64,16},{72,24},{80,32},{88,40},{96,48},{104,56},{11... | collective-permute-start | bytes 786440 | tf_op jit(solution)/shard_map/ppermute | solution.py:28
  352.2 54.6 %all_gather.55 = f32[4,4096]{0,1:T(8,128)S(1)} all-gather(f32[4,256]{0,1:T(8,128)S(1)} %bitcast.376), channel_id=1, replica_groups=mesh['dp'=4,'seq'=16,'head'=8] {'seq'}, dimensions={1}, use_global_device_ids=true | all-gather | bytes 69632 | tf_op jit(solution)/shard_map/all_gather | solution.py:244
  406.8 18.5 %all_gather.54 = f32[4,4096]{1,0:T(4,128)} all-gather(f32[4,256]{1,0:T(4,128)S(1)} %copy-done.30), channel_id=1, replica_groups=mesh['dp'=4,'seq'=16,'head'=8] {'seq'}, dimensions={1}, use_global_device_ids=true | all-gather | bytes 69632 | tf_op jit(solution)/shard_map/all_gather | solution.py:243
  426.3 9.7 %conditional.18 = (f32[256,4,128]{2,0,1:T(8,128)S(1)}, f32[256,4,128]{2,0,1:T(8,128)S(1)}) conditional(s32[]{:T(128)} %convert_element_type.265, (s32[256]{0:T(256)S(1)}, s32[]{:T(128)}, s32[256]{0:T(256)S(1)}, s32[4096]{0:T(1024)}, bf16[256,4,128]{0,2,1:T(8,128)(2,1)}, /*index=5*/bf16[256,4,128]{0,2,1:T(8,128)(2,1)S(1)}, f32[4,4096]{1,0:T(4,128)}, ...), branch_computations={%region_17.18_spmd, %region_18.19_spmd} | conditional | flops 271122688 | bytes 10255450 | solution.py:332
  435.9 8.6 %conditional.19 = ((f32[256,4,128]{2,0,1:T(8,128)S(1)}, f32[256,4,128]{2,0,1:T(8,128)S(1)})) conditional(s32[]{:T(128)} %convert_element_type.264, (s32[256]{0:T(256)S(1)}, s32[]{:T(128)}, s32[256]{0:T(256)S(1)}, s32[4096]{0:T(1024)}, bf16[256,4,128]{0,2,1:T(8,128)(2,1)}, /*index=5*/bf16[256,4,128]{0,2,1:T(8,128)(2,1)}, f32[4,4096]{1,0:T(4,128)}, ...), branch_computations={%region_19.20_spmd, %region_20.21_spmd} | conditional | flops 271122688 | bytes 7109702 | solution.py:332
  444.5 8.6 %conditional.20 = ((f32[256,4,128]{2,0,1:T(8,128)S(1)}, f32[256,4,128]{2,0,1:T(8,128)S(1)})) conditional(s32[]{:T(128)} %convert_element_type.263, (s32[256]{0:T(256)S(1)}, s32[]{:T(128)}, s32[256]{0:T(256)S(1)}, s32[4096]{0:T(1024)}, bf16[256,4,128]{0,2,1:T(8,128)(2,1)}, /*index=5*/bf16[256,4,128]{0,2,1:T(8,128)(2,1)}, f32[4,4096]{1,0:T(4,128)}, ...), branch_computations={%region_21.22_spmd, %region_22.23_spmd} | conditional | flops 271122688 | bytes 7109702 | solution.py:332
  453.1 8.8 %conditional.21 = ((f32[256,4,128]{2,0,1:T(8,128)S(1)}, f32[256,4,128]{2,0,1:T(8,128)S(1)})) conditional(s32[]{:T(128)} %convert_element_type.262, (s32[256]{0:T(256)S(1)}, s32[]{:T(128)}, s32[256]{0:T(256)S(1)}, s32[4096]{0:T(1024)}, bf16[256,4,128]{0,2,1:T(8,128)(2,1)}, /*index=5*/bf16[256,4,128]{0,2,1:T(8,128)(2,1)}, f32[4,4096]{1,0:T(4,128)}, ...), branch_computations={%region_23.24_spmd, %region_24.25_spmd} | conditional | flops 271122688 | bytes 7109702 | solution.py:332
  461.9 8.6 %conditional.22 = ((f32[256,4,128]{2,0,1:T(8,128)S(1)}, f32[256,4,128]{2,0,1:T(8,128)S(1)})) conditional(s32[]{:T(128)} %convert_element_type.261, (s32[256]{0:T(256)S(1)}, s32[]{:T(128)}, s32[256]{0:T(256)S(1)}, s32[4096]{0:T(1024)}, bf16[256,4,128]{0,2,1:T(8,128)(2,1)}, /*index=5*/bf16[256,4,128]{0,2,1:T(8,128)(2,1)}, f32[4,4096]{1,0:T(4,128)}, ...), branch_computations={%region_25.26_spmd, %region_26.27_spmd} | conditional | flops 271122688 | bytes 7109702 | solution.py:332
  470.5 8.6 %conditional.23 = ((f32[256,4,128]{2,0,1:T(8,128)S(1)}, f32[256,4,128]{2,0,1:T(8,128)S(1)})) conditional(s32[]{:T(128)} %convert_element_type.260, (s32[256]{0:T(256)S(1)}, s32[]{:T(128)}, s32[256]{0:T(256)S(1)}, s32[4096]{0:T(1024)}, bf16[256,4,128]{0,2,1:T(8,128)(2,1)}, /*index=5*/bf16[256,4,128]{0,2,1:T(8,128)(2,1)}, f32[4,4096]{1,0:T(4,128)}, ...), branch_computations={%region_27.28_spmd, %region_28.29_spmd} | conditional | flops 271122688 | bytes 7109702 | solution.py:332
  479.1 8.6 %conditional.24 = ((f32[256,4,128]{2,0,1:T(8,128)S(1)}, f32[256,4,128]{2,0,1:T(8,128)S(1)})) conditional(s32[]{:T(128)} %convert_element_type.259, (s32[256]{0:T(256)S(1)}, s32[]{:T(128)}, s32[256]{0:T(256)S(1)}, s32[4096]{0:T(1024)}, bf16[256,4,128]{0,2,1:T(8,128)(2,1)}, /*index=5*/bf16[256,4,128]{0,2,1:T(8,128)(2,1)}, f32[4,4096]{1,0:T(4,128)}, ...), branch_computations={%region_29.30_spmd, %region_30.31_spmd} | conditional | flops 271122688 | bytes 7109702 | solution.py:332
  487.7 8.6 %conditional.25 = ((f32[256,4,128]{2,0,1:T(8,128)S(1)}, f32[256,4,128]{2,0,1:T(8,128)S(1)})) conditional(s32[]{:T(128)} %convert_element_type.258, (s32[256]{0:T(256)S(1)}, s32[]{:T(128)}, s32[256]{0:T(256)S(1)}, s32[4096]{0:T(1024)}, bf16[256,4,128]{0,2,1:T(8,128)(2,1)}, /*index=5*/bf16[256,4,128]{0,2,1:T(8,128)(2,1)}, f32[4,4096]{1,0:T(4,128)}, ...), branch_computations={%region_31.32_spmd, %region_32.33_spmd} | conditional | flops 271122688 | bytes 7109702 | solution.py:332
  504.8 92.7 %while.45 = (s32[]{:T(128)}, f32[4,128,128]{2,1,0:T(8,128)S(1)}, f32[]{:T(128)}, s32[]{:T(128)}, f32[16]{0:T(128)S(1)}, /*index=5*/f32[16]{0:T(128)S(1)}, f32[16...) while((s32[]{:T(128)}, f32[4,128,128]{2,1,0:T(8,128)S(1)}, ...), condition=%wide.region_1.2_spmd, body=%wide.region_0.1_spmd.sunk | while | flops 262154 | bytes 786708 | solution.py:22
  (417 shorter events, 251.5 us)
Async XLA Ops:
  7.2 52.0 %all-gather.15.cloned.1.call-start = ((), (), s32[]{:S(2)}) async-start(), calls=%async_computation.3 | async-start | bytes 4456448 | tf_op jit(solution)/shard_map/all_gather | solution.py:13
  13.0 215.9 %copy-start.7 = (bf16[256,512]{0,1:T(8,128)(2,1)}, bf16[256,512]{0,1:T(8,128)(2,1)S(1)}, u32[]{:S(2)}) copy-start(bf16[256,512]{0,1:T(8,128)(2,1)S(1)} %copy.484) | copy-start | bytes 786436
  14.2 182.3 %copy-start.9 = (bf16[256,512]{0,1:T(8,128)(2,1)}, bf16[256,512]{0,1:T(8,128)(2,1)S(1)}, u32[]{:S(2)}) copy-start(bf16[256,512]{0,1:T(8,128)(2,1)S(1)} %copy.485) | copy-start | bytes 786436
  16.0 182.4 %all-gather.11.cloned.1.call-start = ((), (), s32[]{:S(2)}) async-start(), calls=%async_computation.1 | async-start | bytes 4456448 | tf_op jit(solution)/shard_map/all_gather | solution.py:177
  16.9 181.4 %all-gather.9.cloned.1.call-start = ((), (), s32[]{:S(2)}) async-start(), calls=%async_computation | async-start | bytes 4456448 | tf_op jit(solution)/shard_map/all_gather | solution.py:176
  17.8 486.2 %all-gather.13.cloned.1.call-start = ((), (), s32[]{:S(2)}) async-start(), calls=%async_computation.2 | async-start | bytes 4456448 | tf_op jit(solution)/shard_map/all_gather | solution.py:13
  59.4 137.6 %copy-start.38 = (f32[16]{0:T(128)}, f32[16]{0:T(128)S(1)}, u32[]{:S(2)}) copy-start(f32[16]{0:T(128)S(1)} %get-tuple-element.2860) | copy-start | bytes 196
  62.6 165.0 %collective-permute-start.15 = (bf16[256,512]{0,1:T(8,128)(2,1)}, bf16[256,512]{0,1:T(8,128)(2,1)}, u32[]{:S(2)}, u32[]{:S(2)}) collective-permute-start(bf16[256,512]{0,1:T(8,128)(2,1)} %copy.333), channel_id=1, source_target_pairs={{8,0},{16,8},{24,16},{32,24},{40,32},{48,40},{56,48},{64,56},{72,6... | collective-permute-start | bytes 786440 | tf_op jit(solution)/shard_map/ppermute | solution.py:28
  70.9 176.2 %collective-permute-start.13 = (bf16[256,512]{0,1:T(8,128)(2,1)}, bf16[256,512]{0,1:T(8,128)(2,1)}, u32[]{:S(2)}, u32[]{:S(2)}) collective-permute-start(bf16[256,512]{0,1:T(8,128)(2,1)} %copy.333), channel_id=1, source_target_pairs={{16,0},{24,8},{32,16},{40,24},{48,32},{56,40},{64,48},{72,56},{80,... | collective-permute-start | bytes 786440 | tf_op jit(solution)/shard_map/ppermute | solution.py:28
  85.0 145.0 %collective-permute-start.14 = (bf16[256,512]{0,1:T(8,128)(2,1)}, bf16[256,512]{0,1:T(8,128)(2,1)}, u32[]{:S(2)}, u32[]{:S(2)}) collective-permute-start(bf16[256,512]{0,1:T(8,128)(2,1)} %copy.329), channel_id=1, source_target_pairs={{8,0},{16,8},{24,16},{32,24},{40,32},{48,40},{56,48},{64,56},{72,6... | collective-permute-start | bytes 786440 | tf_op jit(solution)/shard_map/ppermute | solution.py:28
  94.0 155.1 %collective-permute-start.12 = (bf16[256,512]{0,1:T(8,128)(2,1)}, bf16[256,512]{0,1:T(8,128)(2,1)}, u32[]{:S(2)}, u32[]{:S(2)}) collective-permute-start(bf16[256,512]{0,1:T(8,128)(2,1)} %copy.329), channel_id=1, source_target_pairs={{16,0},{24,8},{32,16},{40,24},{48,32},{56,40},{64,48},{72,56},{80,... | collective-permute-start | bytes 786440 | tf_op jit(solution)/shard_map/ppermute | solution.py:28
  107.3 143.7 %collective-permute-start.11 = (bf16[256,512]{0,1:T(8,128)(2,1)}, bf16[256,512]{0,1:T(8,128)(2,1)S(1)}, u32[]{:S(2)}, u32[]{:S(2)}) collective-permute-start(bf16[256,512]{0,1:T(8,128)(2,1)} %copy.333), channel_id=1, source_target_pairs={{24,0},{32,8},{40,16},{48,24},{56,32},{64,40},{72,48},{80,56},{88,... | collective-permute-start | bytes 786440 | tf_op jit(solution)/shard_map/ppermute | solution.py:28
  227.6 25.5 %collective-permute-start.10 = (bf16[256,512]{0,1:T(8,128)(2,1)}, bf16[256,512]{0,1:T(8,128)(2,1)S(1)}, u32[]{:S(2)}, u32[]{:S(2)}) collective-permute-start(bf16[256,512]{0,1:T(8,128)(2,1)} %copy.329), channel_id=1, source_target_pairs={{24,0},{32,8},{40,16},{48,24},{56,32},{64,40},{72,48},{80,56},{88,... | collective-permute-start | bytes 786440 | tf_op jit(solution)/shard_map/ppermute | solution.py:28
  230.0 95.4 %collective-permute-start.9 = (bf16[256,512]{0,1:T(8,128)(2,1)}, bf16[256,512]{0,1:T(8,128)(2,1)}, u32[]{:S(2)}, u32[]{:S(2)}) collective-permute-start(bf16[256,512]{0,1:T(8,128)(2,1)} %copy.333), channel_id=1, source_target_pairs={{32,0},{40,8},{48,16},{56,24},{64,32},{72,40},{80,48},{88,56},{96,... | collective-permute-start | bytes 786440 | tf_op jit(solution)/shard_map/ppermute | solution.py:28
  247.1 95.1 %collective-permute-start.8 = (bf16[256,512]{0,1:T(8,128)(2,1)}, bf16[256,512]{0,1:T(8,128)(2,1)}, u32[]{:S(2)}, u32[]{:S(2)}) collective-permute-start(bf16[256,512]{0,1:T(8,128)(2,1)} %copy.329), channel_id=1, source_target_pairs={{32,0},{40,8},{48,16},{56,24},{64,32},{72,40},{80,48},{88,56},{96,... | collective-permute-start | bytes 786440 | tf_op jit(solution)/shard_map/ppermute | solution.py:28
  249.1 95.1 %collective-permute-start.7 = (bf16[256,512]{0,1:T(8,128)(2,1)}, bf16[256,512]{0,1:T(8,128)(2,1)}, u32[]{:S(2)}, u32[]{:S(2)}) collective-permute-start(bf16[256,512]{0,1:T(8,128)(2,1)} %copy.333), channel_id=1, source_target_pairs={{40,0},{48,8},{56,16},{64,24},{72,32},{80,40},{88,48},{96,56},{104... | collective-permute-start | bytes 786440 | tf_op jit(solution)/shard_map/ppermute | solution.py:28
  251.1 95.1 %collective-permute-start.6 = (bf16[256,512]{0,1:T(8,128)(2,1)}, bf16[256,512]{0,1:T(8,128)(2,1)}, u32[]{:S(2)}, u32[]{:S(2)}) collective-permute-start(bf16[256,512]{0,1:T(8,128)(2,1)} %copy.329), channel_id=1, source_target_pairs={{40,0},{48,8},{56,16},{64,24},{72,32},{80,40},{88,48},{96,56},{104... | collective-permute-start | bytes 786440 | tf_op jit(solution)/shard_map/ppermute | solution.py:28
  253.1 95.1 %collective-permute-start.5 = (bf16[256,512]{0,1:T(8,128)(2,1)}, bf16[256,512]{0,1:T(8,128)(2,1)}, u32[]{:S(2)}, u32[]{:S(2)}) collective-permute-start(bf16[256,512]{0,1:T(8,128)(2,1)} %copy.333), channel_id=1, source_target_pairs={{48,0},{56,8},{64,16},{72,24},{80,32},{88,40},{96,48},{104,56},{11... | collective-permute-start | bytes 786440 | tf_op jit(solution)/shard_map/ppermute | solution.py:28
  325.4 153.7 %collective-permute-start.4 = (bf16[256,512]{0,1:T(8,128)(2,1)}, bf16[256,512]{0,1:T(8,128)(2,1)}, u32[]{:S(2)}, u32[]{:S(2)}) collective-permute-start(bf16[256,512]{0,1:T(8,128)(2,1)} %copy.329), channel_id=1, source_target_pairs={{48,0},{56,8},{64,16},{72,24},{80,32},{88,40},{96,48},{104,56},{11... | collective-permute-start | bytes 786440 | tf_op jit(solution)/shard_map/ppermute | solution.py:28
  342.2 145.6 %collective-permute-start.3 = (bf16[256,512]{0,1:T(8,128)(2,1)}, bf16[256,512]{0,1:T(8,128)(2,1)}, u32[]{:S(2)}, u32[]{:S(2)}) collective-permute-start(bf16[256,512]{0,1:T(8,128)(2,1)} %copy.333), channel_id=1, source_target_pairs={{56,0},{64,8},{72,16},{80,24},{88,32},{96,40},{104,48},{112,56},{1... | collective-permute-start | bytes 786440 | tf_op jit(solution)/shard_map/ppermute | solution.py:28
  344.2 143.6 %collective-permute-start.2 = (bf16[256,512]{0,1:T(8,128)(2,1)}, bf16[256,512]{0,1:T(8,128)(2,1)}, u32[]{:S(2)}, u32[]{:S(2)}) collective-permute-start(bf16[256,512]{0,1:T(8,128)(2,1)} %copy.329), channel_id=1, source_target_pairs={{56,0},{64,8},{72,16},{80,24},{88,32},{96,40},{104,48},{112,56},{1... | collective-permute-start | bytes 786440 | tf_op jit(solution)/shard_map/ppermute | solution.py:28
  346.1 150.2 %collective-permute-start.1 = (bf16[256,512]{0,1:T(8,128)(2,1)}, bf16[256,512]{0,1:T(8,128)(2,1)}, u32[]{:S(2)}, u32[]{:S(2)}) collective-permute-start(bf16[256,512]{0,1:T(8,128)(2,1)} %copy.333), channel_id=1, source_target_pairs={{64,0},{72,8},{80,16},{88,24},{96,32},{104,40},{112,48},{120,56},{... | collective-permute-start | bytes 786440 | tf_op jit(solution)/shard_map/ppermute | solution.py:28
  348.2 148.2 %collective-permute-start = (bf16[256,512]{0,1:T(8,128)(2,1)}, bf16[256,512]{0,1:T(8,128)(2,1)}, u32[]{:S(2)}, u32[]{:S(2)}) collective-permute-start(bf16[256,512]{0,1:T(8,128)(2,1)} %copy.329), channel_id=1, source_target_pairs={{64,0},{72,8},{80,16},{88,24},{96,32},{104,40},{112,48},{120,56},{... | collective-permute-start | bytes 786440 | tf_op jit(solution)/shard_map/ppermute | solution.py:28
  504.1 93.9 %copy-start.8 = (bf16[256,512]{0,1:T(8,128)(2,1)S(1)}, bf16[256,512]{0,1:T(8,128)(2,1)}, u32[]{:S(2)}) copy-start(bf16[256,512]{0,1:T(8,128)(2,1)} %copy-done.7) | copy-start | bytes 786436
  (37 other events, 1030.9 us)
Sparse Core Ops, SparseCore 0:
  16.1 43.0 all-gather.14
  61.3 50.2 all-gather.10
  114.3 61.8 all-gather.8
  178.7 45.7 all-gather.12
where the time goes:
time: 613 us; the launch traced here: 608 us
  blocking collectives  160 us (26%)
  starting transfers between devices  143 us (23%)
  local copies, waits for them, and re-layouts  100 us (16%)
  matrix products  73.8 us (12%)
  loops' own time  70.5 us (12%)
  other arithmetic  29.4 us (5%)
  between operations  16 us (3%)
  waiting for transfers between devices  15.4 us (3%)
    ppermute x16, starting transfers between devices, from_behind(): lax.ppermute(value, axis, [(source, source + steps) for source in range(f...  142 us
    all_gather x1, blocking collectives, per_device(): all_ids = lax.all_gather(doc_ids, 'seq', axis=0, tiled=True)  62.3 us
    all_gather x1, blocking collectives, per_device(): lax.all_gather(delta, 'seq', axis=1, tiled=True)  54.6 us
    another operation x2, loops' own time, entering(): return lax.fori_loop(0, ahead, one, state)  47.9 us
    unnamed x1, blocking collectives  24.3 us
    dot_general x9, matrix products, key_terms(): jnp.einsum('thd,shd->hts', piece_query, soft_keys, preferred_element_type...  21.4 us
    all_gather x1, blocking collectives, per_device(): lax.all_gather(lse, 'seq', axis=1, tiled=True)  18.5 us
    dynamic_slice x30, local copies, waits for them, and re-layouts, one(): lax.dynamic_index_in_dim(a, source, 0, False)  18.4 us
  transfers between devices with their start and end apart: 20, of which 1 were waited for; matrix products, arithmetic and copies ran while one was open for 24% of the time, Pallas kernels for 0%

commit v1 on v0

v1 whole, which is shorter than its diff:
```python
import jax
import jax.numpy as jnp
from jax import lax
from jax.sharding import PartitionSpec as P

PRECISE = lax.Precision.HIGH
REACH = 8


def mixed(form, left, right):
    return jnp.einsum(form, left, right, precision=PRECISE, preferred_element_type=jnp.float32)


def exact(form, left, right):
    return jnp.einsum(form, left, right, preferred_element_type=jnp.float32)


def relay(value, steps, shift):
    count = lax.axis_size("seq")
    pairs = [(s, s + shift) for s in range(count) if 0 <= s + shift < count]
    out = []
    cur = value
    for _ in range(steps):
        cur = lax.ppermute(cur, "seq", pairs)
        out.append(cur)
    return out


def shifted(value, shift):
    count = lax.axis_size("seq")
    pairs = [(s, s + shift) for s in range(count) if 0 <= s + shift < count]
    return lax.ppermute(value, "seq", pairs)


def per_device(
    doc_ids,
    light_q,
    light_k,
    light_v,
    light_decay,
    light_grad_out,
    soft_q,
    soft_k,
    soft_v,
    soft_grad_out,
):
    rows = light_q.shape[0]
    heads = light_decay.shape[0]
    width = light_q.shape[1] // heads
    count = lax.axis_size("seq")
    me = lax.axis_index("seq")
    total_rows = rows * count
    reach = min(REACH, count - 1)
    span = (reach + 1) * rows
    scale = width ** (-0.5)

    all_ids = lax.all_gather(doc_ids, "seq", axis=0, tiled=True)
    local = jnp.arange(rows, dtype=jnp.int32)
    positions = me * rows + local
    head_id = doc_ids[0]
    tail_id = doc_ids[-1]
    slope = light_decay

    def shape3(a):
        return a.reshape(rows, heads, width)

    lq, lk, lv, ldo = shape3(light_q), shape3(light_k), shape3(light_v), shape3(light_grad_out)
    sq, sk, sv, sdo = shape3(soft_q), shape3(soft_k), shape3(soft_v), shape3(soft_grad_out)
    lqf, lkf, lvf, ldof = (a.astype(jnp.float32) for a in (lq, lk, lv, ldo))

    since_start = (local + 1).astype(jnp.float32)
    until_end = (rows - 1 - local).astype(jnp.float32)
    start_decay = jnp.exp(-since_start[:, None] * slope[None, :])
    end_decay = jnp.exp(-until_end[:, None] * slope[None, :])
    tail_part = end_decay * (doc_ids == tail_id)[:, None]
    head_part = start_decay * (doc_ids == head_id)[:, None]
    send_state = mixed("shk,shv->hkv", lkf * tail_part[:, :, None], lvf)
    back_state = mixed("thq,tho->hqo", lqf * head_part[:, :, None], ldof)

    fwd = relay((jnp.concatenate([soft_k, soft_v], axis=1), send_state), reach, 1)
    bwd = relay((jnp.concatenate([soft_q, soft_grad_out], axis=1), back_state), reach, -1)

    inside = (doc_ids[:, None] == doc_ids[None, :]) & (local[None, :] <= local[:, None])
    distance = jnp.maximum(local[:, None] - local[None, :], 0).astype(jnp.float32)
    weight = jnp.where(inside[None], jnp.exp(-slope[:, None, None] * distance[None]), 0.0)
    scores = exact("thd,shd->hts", lq, lk) * weight
    grad_scores = exact("thv,shv->hts", ldo, lv) * weight
    light_out = mixed("hts,shd->thd", scores, lvf)
    light_dq = mixed("hts,shk->thk", grad_scores, lkf)
    light_dk = mixed("hts,thk->shk", grad_scores, lqf)
    light_dv = mixed("hts,thv->shv", scores, ldof)

    keep = jnp.exp(-slope * rows)
    inherited = jnp.zeros_like(send_state)
    for k in range(1, reach + 1):
        source = me - k
        source_tail = all_ids[jnp.clip(source * rows + rows - 1, 0, total_rows - 1)]
        use = (source >= 0) & (source_tail == head_id)
        factor = jnp.where(use, keep ** (k - 1), 0.0)
        inherited = inherited + factor[:, None, None] * fwd[k - 1][1]
    ahead = jnp.zeros_like(back_state)
    for k in range(1, reach + 1):
        source = me + k
        source_head = all_ids[jnp.clip(source * rows, 0, total_rows - 1)]
        use = (source < count) & (source_head == tail_id)
        factor = jnp.where(use, keep ** (k - 1), 0.0)
        ahead = ahead + factor[:, None, None] * bwd[k - 1][1]
    light_out = light_out + mixed("thk,hkv->thv", lqf * head_part[:, :, None], inherited)
    light_dq = light_dq + mixed("thv,hkv->thk", ldof * head_part[:, :, None], inherited)
    light_dk = light_dk + mixed("hqo,sho->shq", ahead, lvf) * tail_part[:, :, None]
    light_dv = light_dv + mixed("hqo,shq->sho", ahead, lkf) * tail_part[:, :, None]

    key_blocks = [jnp.concatenate([soft_k, soft_v], axis=1)] + [f[0] for f in fwd]
    key_all = jnp.concatenate(key_blocks[::-1], axis=0)
    keys = key_all[:, : heads * width].reshape(span, heads, width)
    values = key_all[:, heads * width :].reshape(span, heads, width)
    key_pos = (me - reach) * rows + jnp.arange(span, dtype=jnp.int32)
    key_ids = all_ids[jnp.clip(key_pos, 0, total_rows - 1)]
    allowed = (
        (key_pos[None, :] >= 0)
        & (key_pos[None, :] <= positions[:, None])
        & (key_ids[None, :] == doc_ids[:, None])
    )[None]
    logits = exact("thd,shd->hts", sq, keys) * scale
    masked = jnp.where(allowed, logits, -1e30)
    top = jnp.max(masked, axis=2)
    raw = jnp.where(allowed, jnp.exp(masked - top[:, :, None]), 0.0)
    total = jnp.sum(raw, axis=2)
    accum = exact("hts,shd->htd", raw.astype(jnp.bfloat16), values)
    soft_out = jnp.transpose(accum / total[:, :, None], (1, 0, 2)).astype(jnp.bfloat16)
    lse = top + jnp.log(total)
    delta = jnp.sum(sdo.astype(jnp.float32) * soft_out.astype(jnp.float32), axis=2).T
    prob = jnp.where(allowed, jnp.exp(jnp.where(allowed, logits - lse[:, :, None], -1e30)), 0.0)
    dprob = exact("thd,shd->hts", sdo, values)
    dlogit = (prob * (dprob - delta[:, :, None])).astype(jnp.bfloat16)
    soft_dq = exact("hts,shd->thd", dlogit, keys) * scale

    stats = jnp.stack([lse, delta])
    stat_blocks = [stats] + [shifted(stats, -k) for k in range(1, reach + 1)]
    query_blocks = [jnp.concatenate([soft_q, soft_grad_out], axis=1)] + [b[0] for b in bwd]
    query_all = jnp.concatenate(query_blocks, axis=0)
    queries = query_all[:, : heads * width].reshape(span, heads, width)
    grads = query_all[:, heads * width :].reshape(span, heads, width)
    stat_all = jnp.concatenate(stat_blocks, axis=2)
    lse_all, delta_all = stat_all[0], stat_all[1]
    query_pos = me * rows + jnp.arange(span, dtype=jnp.int32)
    query_ids = all_ids[jnp.clip(query_pos, 0, total_rows - 1)]
    seen = (
        (query_pos[:, None] < total_rows)
        & (positions[None, :] <= query_pos[:, None])
        & (doc_ids[None, :] == query_ids[:, None])
    )[None]
    logits_t = exact("thd,shd->hts", queries, sk) * scale
    prob_t = jnp.where(seen, jnp.exp(jnp.where(seen, logits_t - lse_all[:, :, None], -1e30)), 0.0)
    soft_dv = exact("hts,thd->shd", prob_t.astype(jnp.bfloat16), grads)
    dprob_t = exact("thd,shd->hts", grads, sv)
    dlogit_t = (prob_t * (dprob_t - delta_all[:, :, None])).astype(jnp.bfloat16)
    soft_dk = exact("hts,thd->shd", dlogit_t, queries) * scale

    flat = (rows, heads * width)
    return (
        light_out.reshape(flat).astype(jnp.bfloat16),
        light_dq.reshape(flat).astype(jnp.bfloat16),
        light_dk.reshape(flat).astype(jnp.bfloat16),
        light_dv.reshape(flat).astype(jnp.bfloat16),
        soft_out.reshape(flat),
        soft_dq.reshape(flat).astype(jnp.bfloat16),
        soft_dk.reshape(flat).astype(jnp.bfloat16),
        soft_dv.reshape(flat).astype(jnp.bfloat16),
    )


def solution(mesh):
    row = P(("dp", "seq"), "head")
    return jax.shard_map(
        per_device,
        mesh=mesh,
        in_specs=(P(("dp", "seq")), row, row, row, P("head"), row, row, row, row, row),
        out_specs=(row,) * 8,
        check_vma=False,
    )
```

time: 613 us -> 305 us (0.50)
  the two profiles are of different devices: /device:TPU:455 before, /device:TPU:1 now
where the time goes in v1:
time: 305 us; the launch traced here: 302 us
  starting transfers between devices  105 us (34%)
  local copies, waits for them, and re-layouts  74.1 us (24%)
  matrix products  34.8 us (11%)
  waiting for transfers between devices  31.6 us (10%)
  between operations  21.5 us (7%)
  blocking collectives  20.6 us (7%)
  other arithmetic  14.8 us (5%)
    ppermute x32, starting transfers between devices, relay(): cur = lax.ppermute(cur, 'seq', pairs)  94 us
    unnamed x81, local copies, waits for them, and re-layouts  37.5 us
    dot_general x8, matrix products, exact(): return jnp.einsum(form, left, right, preferred_element_type=jnp.float32)  28.9 us
    all_gather x1, blocking collectives, per_device(): all_ids = lax.all_gather(doc_ids, 'seq', axis=0, tiled=True)  20.6 us
    ppermute x8, waiting for transfers between devices, shifted(): return lax.ppermute(value, 'seq', pairs)  19.8 us
    gather x1, local copies, waits for them, and re-layouts, per_device(): key_ids = all_ids[jnp.clip(key_pos, 0, total_rows - 1)]  12.3 us
    gather x1, local copies, waits for them, and re-layouts, per_device(): query_ids = all_ids[jnp.clip(query_pos, 0, total_rows - 1)]  12.3 us
    ppermute x32, waiting for transfers between devices, relay(): cur = lax.ppermute(cur, 'seq', pairs)  11.7 us
  transfers between devices with their start and end apart: 40, of which 9 were waited for; matrix products, arithmetic and copies ran while one was open for 32% of the time, Pallas kernels for 0%

profile of v1, /device:TPU:1, one launch (start us, length us, event | category | flops | bytes accessed | tf_op | source)
XLA Modules:
  0.0 302.4 jit_solution(12735984447254743109)
XLA Ops:
  6.8 5.4 %collective-permute-start = (f32[4,128,128]{2,1,0:T(8,128)}, f32[4,128,128]{2,1,0:T(8,128)}, u32[]{:S(2)}, u32[]{:S(2)}) collective-permute-start(f32[4,128,128]{2,1,0:T(8,128)} %fusion.43), channel_id=1, source_target_pairs={{0,8},{8,16},{16,24},{24,32},{32,40},{40,48},{48,56},{56,64},{64,7... | collective-permute-start | bytes 786440 | tf_op jit(solution)/shard_map/ppermute | solution.py:24
  15.4 5.4 %collective-permute-start.8 = (f32[4,128,128]{2,1,0:T(8,128)}, f32[4,128,128]{2,1,0:T(8,128)}, u32[]{:S(2)}, u32[]{:S(2)}) collective-permute-start(f32[4,128,128]{2,1,0:T(8,128)} %fusion.42), channel_id=1, source_target_pairs={{8,0},{16,8},{24,16},{32,24},{40,32},{48,40},{56,48},{64,56},{72,6... | collective-permute-start | bytes 786440 | tf_op jit(solution)/shard_map/ppermute | solution.py:24
  30.3 20.6 %all-gather = s32[16,1,256]{2,1,0:T(1,128)S(1)} all-gather(s32[1,1,256]{2,1,0:T(1,128)S(1)} %bitcast.242), channel_id=1, replica_groups=mesh['dp'=4,'seq'=16,'head'=8] {'seq'}, dimensions={0}, use_global_device_ids=true | all-gather | bytes 17408 | tf_op jit(solution)/shard_map/all_gather | solution.py:57
  68.8 12.3 %gather_fusion = s32[2304]{0:T(1024)S(1)} fusion(s32[4096]{0:T(1024)S(1)} %bitcast.211, s32[3072]{0:T(1024)S(1)} %get-tuple-element.94), kind=kCustom, calls=%fused_computation | custom fusion | bytes 27648 | tf_op jit(solution)/shard_map/gather | solution.py:118
  81.2 12.3 %gather_fusion.1 = s32[2304]{0:T(1024)S(1)} fusion(s32[4096]{0:T(1024)S(1)} %bitcast.212, s32[3072]{0:T(1024)S(1)} %get-tuple-element.93), kind=kCustom, calls=%fused_computation.1 | custom fusion | bytes 27648 | tf_op jit(solution)/shard_map/gather | solution.py:147
  110.9 4.3 %collective-permute-start.2 = (f32[4,128,128]{2,1,0:T(8,128)S(1)}, f32[4,128,128]{2,1,0:T(8,128)S(1)}, u32[]{:S(2)}, u32[]{:S(2)}) collective-permute-start(f32[4,128,128]{2,1,0:T(8,128)S(1)} %collective-permute-done.1), channel_id=1, source_target_pairs={{0,8},{8,16},{16,24},{24,32},{32,40},{40,48},{48,56},{56,64},{64,7... | collective-permute-start | bytes 786440 | tf_op jit(solution)/shard_map/ppermute | solution.py:24
  117.1 3.6 %collective-permute-start.18 = (bf16[256,1024]{0,1:T(8,128)(2,1)}, bf16[256,1024]{0,1:T(8,128)(2,1)S(1)}, u32[]{:S(2)}, u32[]{:S(2)}) collective-permute-start(bf16[256,1024]{0,1:T(8,128)(2,1)} %collective-permute-done.17), channel_id=1, source_target_pairs={{0,8},{8,16},{16,24},{24,32},{32,40},{40,48},{48,56},{56,64},{64,7... | collective-permute-start | bytes 1572872 | tf_op jit(solution)/shard_map/ppermute | solution.py:24
  123.1 3.6 %collective-permute-start.3 = (f32[4,128,128]{2,1,0:T(8,128)S(1)}, f32[4,128,128]{2,1,0:T(8,128)S(1)}, u32[]{:S(2)}, u32[]{:S(2)}) collective-permute-start(f32[4,128,128]{2,1,0:T(8,128)S(1)} %collective-permute-done.2), channel_id=1, source_target_pairs={{0,8},{8,16},{16,24},{24,32},{32,40},{40,48},{48,56},{56,64},{64,7... | collective-permute-start | bytes 786440 | tf_op jit(solution)/shard_map/ppermute | solution.py:24
  130.8 3.6 %collective-permute-start.4 = (f32[4,128,128]{2,1,0:T(8,128)S(1)}, f32[4,128,128]{2,1,0:T(8,128)S(1)}, u32[]{:S(2)}, u32[]{:S(2)}) collective-permute-start(f32[4,128,128]{2,1,0:T(8,128)S(1)} %collective-permute-done.3), channel_id=1, source_target_pairs={{0,8},{8,16},{16,24},{24,32},{32,40},{40,48},{48,56},{56,64},{64,7... | collective-permute-start | bytes 786440 | tf_op jit(solution)/shard_map/ppermute | solution.py:24
  136.4 3.6 %collective-permute-start.19 = (bf16[256,1024]{0,1:T(8,128)(2,1)S(1)}, bf16[256,1024]{0,1:T(8,128)(2,1)S(1)}, u32[]{:S(2)}, u32[]{:S(2)}) collective-permute-start(bf16[256,1024]{0,1:T(8,128)(2,1)S(1)} %collective-permute-done.18), channel_id=1, source_target_pairs={{0,8},{8,16},{16,24},{24,32},{32,40},{40,48},{48,56},{56,64},{64,7... | collective-permute-start | bytes 1572872 | tf_op jit(solution)/shard_map/ppermute | solution.py:24
  142.4 3.6 %collective-permute-start.5 = (f32[4,128,128]{2,1,0:T(8,128)S(1)}, f32[4,128,128]{2,1,0:T(8,128)S(1)}, u32[]{:S(2)}, u32[]{:S(2)}) collective-permute-start(f32[4,128,128]{2,1,0:T(8,128)S(1)} %collective-permute-done.4), channel_id=1, source_target_pairs={{0,8},{8,16},{16,24},{24,32},{32,40},{40,48},{48,56},{56,64},{64,7... | collective-permute-start | bytes 786440 | tf_op jit(solution)/shard_map/ppermute | solution.py:24
  152.0 3.6 %collective-permute-start.6 = (f32[4,128,128]{2,1,0:T(8,128)S(1)}, f32[4,128,128]{2,1,0:T(8,128)S(1)}, u32[]{:S(2)}, u32[]{:S(2)}) collective-permute-start(f32[4,128,128]{2,1,0:T(8,128)S(1)} %collective-permute-done.5), channel_id=1, source_target_pairs={{0,8},{8,16},{16,24},{24,32},{32,40},{40,48},{48,56},{56,64},{64,7... | collective-permute-start | bytes 786440 | tf_op jit(solution)/shard_map/ppermute | solution.py:24
  160.9 3.6 %collective-permute-start.7 = (f32[4,128,128]{2,1,0:T(8,128)S(1)}, f32[4,128,128]{2,1,0:T(8,128)S(1)}, u32[]{:S(2)}, u32[]{:S(2)}) collective-permute-start(f32[4,128,128]{2,1,0:T(8,128)S(1)} %collective-permute-done.6), channel_id=1, source_target_pairs={{0,8},{8,16},{16,24},{24,32},{32,40},{40,48},{48,56},{56,64},{64,7... | collective-permute-start | bytes 786440 | tf_op jit(solution)/shard_map/ppermute | solution.py:24
  172.2 5.6 %collective-permute-start.21 = (bf16[256,1024]{0,1:T(8,128)(2,1)S(1)}, bf16[256,1024]{0,1:T(8,128)(2,1)S(1)}, u32[]{:S(2)}, u32[]{:S(2)}) collective-permute-start(bf16[256,1024]{0,1:T(8,128)(2,1)S(1)} %collective-permute-done.20), channel_id=1, source_target_pairs={{0,8},{8,16},{16,24},{24,32},{32,40},{40,48},{48,56},{56,64},{64,7... | collective-permute-start | bytes 1572872 | tf_op jit(solution)/shard_map/ppermute | solution.py:24
  180.2 3.4 %collective-permute-done.28 = bf16[256,1024]{0,1:T(8,128)(2,1)S(1)} collective-permute-done((bf16[256,1024]{0,1:T(8,128)(2,1)S(1)}, bf16[256,1024]{0,1:T(8,128)(2,1)S(1)}, u32[]{:S(2)}, u32[]{:S(2)}) %collective-permute-start.28) | collective-permute-done | bytes 524320 | tf_op jit(solution)/shard_map/ppermute | solution.py:24
  185.5 3.6 %collective-permute-start.22 = (bf16[256,1024]{0,1:T(8,128)(2,1)S(1)}, bf16[256,1024]{0,1:T(8,128)(2,1)}, u32[]{:S(2)}, u32[]{:S(2)}) collective-permute-start(bf16[256,1024]{0,1:T(8,128)(2,1)S(1)} %collective-permute-done.21), channel_id=1, source_target_pairs={{0,8},{8,16},{16,24},{24,32},{32,40},{40,48},{48,56},{56,64},{64,7... | collective-permute-start | bytes 1572872 | tf_op jit(solution)/shard_map/ppermute | solution.py:24
  196.1 3.8 %collective-permute-start.23 = (bf16[256,1024]{0,1:T(8,128)(2,1)}, bf16[256,1024]{0,1:T(8,128)(2,1)}, u32[]{:S(2)}, u32[]{:S(2)}) collective-permute-start(bf16[256,1024]{0,1:T(8,128)(2,1)} %collective-permute-done.22), channel_id=1, source_target_pairs={{0,8},{8,16},{16,24},{24,32},{32,40},{40,48},{48,56},{56,64},{64,7... | collective-permute-start | bytes 1572872 | tf_op jit(solution)/shard_map/ppermute | solution.py:24
  224.9 4.3 %multiply_reduce_fusion = (f32[256,4]{0,1:T(4,128)S(1)}, bf16[256,4,128]{0,2,1:T(8,128)(2,1)}) fusion(bf16[256,512]{0,1:T(8,128)(2,1)S(1)} %copy-done.7, f32[256,4]{0,1:T(4,128)S(1)} %bitcast.243, bf16[2304,4,128]{0,2,1:T(8,128)(2,1)S(1)} %bitcast.231, f32[4,2304,256]{2,1,0:T(8,128)S(1)} %get-tuple-element.88, f32[4,256]{1,0:T(4,128)S(1)} %get-tuple-element.87, ...), kind=kOutput, calls=%fused_computation.54 | convolution fusion | flops 616561664 | bytes 12922880 | tf_op jit(solution)/shard_map/hts,shd->htd/dot_general | solution.py:15
  235.9 9.2 %fusion.33 = bf16[4,128,256]{2,1,0:T(8,128)(2,1)} fusion(bf16[2304,4,128]{0,2,1:T(8,128)(2,1)S(1)} %bitcast.218, f32[4,2304,256]{2,1,0:T(8,128)} %copy-done.1, bf16[2304,4,128]{0,2,1:T(8,128)(2,1)} %bitcast.232, bf16[256,4,128]{0,2,1:T(8,128)(2,1)S(1)} %bitcast.239, f32[4,256]{1,0:T(4,128)S(1)} %bitcast.246, f32[4,256]{1,0:T(4,128)S(1)} %log_add_fusion, ...), kind=kOutput, calls=%fused_computation.48 | convolution fusion | flops 1224736768 | bytes 15278080 | tf_op jit(solution)/shard_map/hts,shd->thd/dot_general | solution.py:15
  248.3 4.1 %fusion.76 = (bf16[2304,512]{0,1:T(8,128)(2,1)S(1)}, bf16[2304,512]{0,1:T(8,128)(2,1)}) fusion(bf16[2304,1024]{0,1:T(8,128)(2,1)} %constant_dynamic-update-slice_fusion.9), kind=kLoop, calls=%fused_computation.157 | loop fusion | bytes 9437184 | tf_op jit(solution)/shard_map/slice | solution.py:143
  264.1 13.2 %collective-permute-done.37 = f32[2,4,256]{2,1,0:T(4,128)S(1)} collective-permute-done((f32[2,4,256]{2,1,0:T(4,128)S(1)}, f32[2,4,256]{2,1,0:T(4,128)S(1)}, u32[]{:S(2)}, u32[]{:S(2)}) %collective-permute-start.37) | collective-permute-done | bytes 8224 | tf_op jit(solution)/shard_map/ppermute | solution.py:32
  278.0 4.9 %collective-permute-done.38 = f32[2,4,256]{2,1,0:T(4,128)S(1)} collective-permute-done((f32[2,4,256]{2,1,0:T(4,128)S(1)}, f32[2,4,256]{2,1,0:T(4,128)S(1)}, u32[]{:S(2)}, u32[]{:S(2)}) %collective-permute-start.38) | collective-permute-done | bytes 8224 | tf_op jit(solution)/shard_map/ppermute | solution.py:32
  285.3 4.8 %exponential_select_fusion = f32[4,2304,256]{2,1,0:T(8,128)S(1)} fusion(bf16[2304,4,128]{0,2,1:T(8,128)(2,1)} %bitcast.215, f32[4,2304]{1,0:T(4,128)S(1)} %get-tuple-element.47, pred[2304,256]{1,0:T(8,128)(4,1)S(1)} %copy-done.8, bf16[256,512]{1,0:T(8,128)(2,1)S(1)} %copy-done.20), kind=kOutput, calls=%fused_computation.10 | convolution fusion | flops 613416960 | bytes 12685312 | tf_op jit(solution)/shard_map/thd,shd->hts/dot_general | solution.py:15
  293.8 7.0 %fusion.29 = bf16[4,128,256]{2,1,0:T(8,128)(2,1)S(1)} fusion(bf16[2304,4,128]{0,2,1:T(8,128)(2,1)} %bitcast.216, f32[4,2304,256]{2,1,0:T(8,128)} %copy-done.2, bf16[2304,4,128]{0,2,1:T(8,128)(2,1)S(1)} %bitcast.214, f32[4,2304]{1,0:T(4,128)S(1)} %get-tuple-element.46, bf16[256,512]{1,0:T(8,128)(2,1)S(1)} %copy-done.4), kind=kOutput, calls=%fused_computation.46 | convolution fusion | flops 1215299584 | bytes 14716928 | tf_op jit(solution)/shard_map/hts,thd->shd/dot_general | solution.py:15
  (191 shorter events, 131.2 us)
Async XLA Ops:
  6.8 97.4 %collective-permute-start = (f32[4,128,128]{2,1,0:T(8,128)}, f32[4,128,128]{2,1,0:T(8,128)}, u32[]{:S(2)}, u32[]{:S(2)}) collective-permute-start(f32[4,128,128]{2,1,0:T(8,128)} %fusion.43), channel_id=1, source_target_pairs={{0,8},{8,16},{16,24},{24,32},{32,40},{40,48},{48,56},{56,64},{64,7... | collective-permute-start | bytes 786440 | tf_op jit(solution)/shard_map/ppermute | solution.py:24
  15.4 91.5 %collective-permute-start.8 = (f32[4,128,128]{2,1,0:T(8,128)}, f32[4,128,128]{2,1,0:T(8,128)}, u32[]{:S(2)}, u32[]{:S(2)}) collective-permute-start(f32[4,128,128]{2,1,0:T(8,128)} %fusion.42), channel_id=1, source_target_pairs={{8,0},{16,8},{24,16},{32,24},{40,32},{48,40},{56,48},{64,56},{72,6... | collective-permute-start | bytes 786440 | tf_op jit(solution)/shard_map/ppermute | solution.py:24
  23.7 74.7 %collective-permute-start.16 = (bf16[256,1024]{0,1:T(8,128)(2,1)}, bf16[256,1024]{0,1:T(8,128)(2,1)}, u32[]{:S(2)}, u32[]{:S(2)}) collective-permute-start(bf16[256,1024]{0,1:T(8,128)(2,1)} %pad_maximum_fusion), channel_id=1, source_target_pairs={{0,8},{8,16},{16,24},{24,32},{32,40},{40,48},{48,56},{56,64},{64,7... | collective-permute-start | bytes 1572872 | tf_op jit(solution)/shard_map/ppermute | solution.py:24
  26.9 88.3 %collective-permute-start.24 = (bf16[256,1024]{0,1:T(8,128)(2,1)S(1)}, bf16[256,1024]{0,1:T(8,128)(2,1)}, u32[]{:S(2)}, u32[]{:S(2)}) collective-permute-start(bf16[256,1024]{0,1:T(8,128)(2,1)S(1)} %get-tuple-element.44), channel_id=1, source_target_pairs={{8,0},{16,8},{24,16},{32,24},{40,32},{48,40},{56,48},{64,56},{72,6... | collective-permute-start | bytes 1572872 | tf_op jit(solution)/shard_map/ppermute | solution.py:24
  98.5 18.6 %collective-permute-start.17 = (bf16[256,1024]{0,1:T(8,128)(2,1)}, bf16[256,1024]{0,1:T(8,128)(2,1)}, u32[]{:S(2)}, u32[]{:S(2)}) collective-permute-start(bf16[256,1024]{0,1:T(8,128)(2,1)} %collective-permute-done.16), channel_id=1, source_target_pairs={{0,8},{8,16},{16,24},{24,32},{32,40},{40,48},{48,56},{56,64},{64,7... | collective-permute-start | bytes 1572872 | tf_op jit(solution)/shard_map/ppermute | solution.py:24
  106.9 14.3 %collective-permute-start.9 = (f32[4,128,128]{2,1,0:T(8,128)}, f32[4,128,128]{2,1,0:T(8,128)S(1)}, u32[]{:S(2)}, u32[]{:S(2)}) collective-permute-start(f32[4,128,128]{2,1,0:T(8,128)} %collective-permute-done.8), channel_id=1, source_target_pairs={{8,0},{16,8},{24,16},{32,24},{40,32},{48,40},{56,48},{64,56},{72,6... | collective-permute-start | bytes 786440 | tf_op jit(solution)/shard_map/ppermute | solution.py:24
  115.2 19.3 %collective-permute-start.25 = (bf16[256,1024]{0,1:T(8,128)(2,1)}, bf16[256,1024]{0,1:T(8,128)(2,1)S(1)}, u32[]{:S(2)}, u32[]{:S(2)}) collective-permute-start(bf16[256,1024]{0,1:T(8,128)(2,1)} %collective-permute-done.24), channel_id=1, source_target_pairs={{8,0},{16,8},{24,16},{32,24},{40,32},{48,40},{56,48},{64,56},{72,6... | collective-permute-start | bytes 1572872 | tf_op jit(solution)/shard_map/ppermute | solution.py:24
  117.1 19.3 %collective-permute-start.18 = (bf16[256,1024]{0,1:T(8,128)(2,1)}, bf16[256,1024]{0,1:T(8,128)(2,1)S(1)}, u32[]{:S(2)}, u32[]{:S(2)}) collective-permute-start(bf16[256,1024]{0,1:T(8,128)(2,1)} %collective-permute-done.17), channel_id=1, source_target_pairs={{0,8},{8,16},{16,24},{24,32},{32,40},{40,48},{48,56},{56,64},{64,7... | collective-permute-start | bytes 1572872 | tf_op jit(solution)/shard_map/ppermute | solution.py:24
  134.4 15.6 %collective-permute-start.26 = (bf16[256,1024]{0,1:T(8,128)(2,1)S(1)}, bf16[256,1024]{0,1:T(8,128)(2,1)S(1)}, u32[]{:S(2)}, u32[]{:S(2)}) collective-permute-start(bf16[256,1024]{0,1:T(8,128)(2,1)S(1)} %collective-permute-done.25), channel_id=1, source_target_pairs={{8,0},{16,8},{24,16},{32,24},{40,32},{48,40},{56,48},{64,56},{72,6... | collective-permute-start | bytes 1572872 | tf_op jit(solution)/shard_map/ppermute | solution.py:24
  136.4 19.2 %collective-permute-start.19 = (bf16[256,1024]{0,1:T(8,128)(2,1)S(1)}, bf16[256,1024]{0,1:T(8,128)(2,1)S(1)}, u32[]{:S(2)}, u32[]{:S(2)}) collective-permute-start(bf16[256,1024]{0,1:T(8,128)(2,1)S(1)} %collective-permute-done.18), channel_id=1, source_target_pairs={{0,8},{8,16},{16,24},{24,32},{32,40},{40,48},{48,56},{56,64},{64,7... | collective-permute-start | bytes 1572872 | tf_op jit(solution)/shard_map/ppermute | solution.py:24
  150.0 20.2 %collective-permute-start.27 = (bf16[256,1024]{0,1:T(8,128)(2,1)S(1)}, bf16[256,1024]{0,1:T(8,128)(2,1)S(1)}, u32[]{:S(2)}, u32[]{:S(2)}) collective-permute-start(bf16[256,1024]{0,1:T(8,128)(2,1)S(1)} %collective-permute-done.26), channel_id=1, source_target_pairs={{8,0},{16,8},{24,16},{32,24},{40,32},{48,40},{56,48},{64,56},{72,6... | collective-permute-start | bytes 1572872 | tf_op jit(solution)/shard_map/ppermute | solution.py:24
  155.7 16.5 %collective-permute-start.20 = (bf16[256,1024]{0,1:T(8,128)(2,1)S(1)}, bf16[256,1024]{0,1:T(8,128)(2,1)S(1)}, u32[]{:S(2)}, u32[]{:S(2)}) collective-permute-start(bf16[256,1024]{0,1:T(8,128)(2,1)S(1)} %collective-permute-done.19), channel_id=1, source_target_pairs={{0,8},{8,16},{16,24},{24,32},{32,40},{40,48},{48,56},{56,64},{64,7... | collective-permute-start | bytes 1572872 | tf_op jit(solution)/shard_map/ppermute | solution.py:24
  160.9 16.9 %collective-permute-start.7 = (f32[4,128,128]{2,1,0:T(8,128)S(1)}, f32[4,128,128]{2,1,0:T(8,128)S(1)}, u32[]{:S(2)}, u32[]{:S(2)}) collective-permute-start(f32[4,128,128]{2,1,0:T(8,128)S(1)} %collective-permute-done.6), channel_id=1, source_target_pairs={{0,8},{8,16},{16,24},{24,32},{32,40},{40,48},{48,56},{56,64},{64,7... | collective-permute-start | bytes 786440 | tf_op jit(solution)/shard_map/ppermute | solution.py:24
  194.2 16.4 %collective-permute-start.30 = (bf16[256,1024]{0,1:T(8,128)(2,1)}, bf16[256,1024]{0,1:T(8,128)(2,1)}, u32[]{:S(2)}, u32[]{:S(2)}) collective-permute-start(bf16[256,1024]{0,1:T(8,128)(2,1)} %collective-permute-done.29), channel_id=1, source_target_pairs={{8,0},{16,8},{24,16},{32,24},{40,32},{48,40},{56,48},{64,56},{72,6... | collective-permute-start | bytes 1572872 | tf_op jit(solution)/shard_map/ppermute | solution.py:24
  196.1 18.3 %collective-permute-start.23 = (bf16[256,1024]{0,1:T(8,128)(2,1)}, bf16[256,1024]{0,1:T(8,128)(2,1)}, u32[]{:S(2)}, u32[]{:S(2)}) collective-permute-start(bf16[256,1024]{0,1:T(8,128)(2,1)} %collective-permute-done.22), channel_id=1, source_target_pairs={{0,8},{8,16},{16,24},{24,32},{32,40},{40,48},{48,56},{56,64},{64,7... | collective-permute-start | bytes 1572872 | tf_op jit(solution)/shard_map/ppermute | solution.py:24
  210.5 34.6 %collective-permute-start.31 = (bf16[256,1024]{0,1:T(8,128)(2,1)}, bf16[256,1024]{0,1:T(8,128)(2,1)}, u32[]{:S(2)}, u32[]{:S(2)}) collective-permute-start(bf16[256,1024]{0,1:T(8,128)(2,1)} %collective-permute-done.30), channel_id=1, source_target_pairs={{8,0},{16,8},{24,16},{32,24},{40,32},{48,40},{56,48},{64,56},{72,6... | collective-permute-start | bytes 1572872 | tf_op jit(solution)/shard_map/ppermute | solution.py:24
  229.9 26.2 %collective-permute-start.32 = (f32[2,4,256]{2,1,0:T(4,128)S(1)}, f32[2,4,256]{2,1,0:T(4,128)S(1)}, u32[]{:S(2)}, u32[]{:S(2)}) collective-permute-start(f32[2,4,256]{2,1,0:T(4,128)S(1)} %get-tuple-element.64), channel_id=1, source_target_pairs={{8,0},{16,8},{24,16},{32,24},{40,32},{48,40},{56,48},{64,56},{72,6... | collective-permute-start | bytes 24584 | tf_op jit(solution)/shard_map/ppermute | solution.py:32
  231.8 26.2 %collective-permute-start.33 = (f32[2,4,256]{2,1,0:T(4,128)S(1)}, f32[2,4,256]{2,1,0:T(4,128)S(1)}, u32[]{:S(2)}, u32[]{:S(2)}) collective-permute-start(f32[2,4,256]{2,1,0:T(4,128)S(1)} %get-tuple-element.64), channel_id=1, source_target_pairs={{16,0},{24,8},{32,16},{40,24},{48,32},{56,40},{64,48},{72,56},{80,... | collective-permute-start | bytes 24584 | tf_op jit(solution)/shard_map/ppermute | solution.py:32
  233.1 26.8 %collective-permute-start.34 = (f32[2,4,256]{2,1,0:T(4,128)S(1)}, f32[2,4,256]{2,1,0:T(4,128)S(1)}, u32[]{:S(2)}, u32[]{:S(2)}) collective-permute-start(f32[2,4,256]{2,1,0:T(4,128)S(1)} %get-tuple-element.64), channel_id=1, source_target_pairs={{24,0},{32,8},{40,16},{48,24},{56,32},{64,40},{72,48},{80,56},{88,... | collective-permute-start | bytes 24584 | tf_op jit(solution)/shard_map/ppermute | solution.py:32
  234.4 27.3 %collective-permute-start.35 = (f32[2,4,256]{2,1,0:T(4,128)S(1)}, f32[2,4,256]{2,1,0:T(4,128)S(1)}, u32[]{:S(2)}, u32[]{:S(2)}) collective-permute-start(f32[2,4,256]{2,1,0:T(4,128)S(1)} %get-tuple-element.64), channel_id=1, source_target_pairs={{32,0},{40,8},{48,16},{56,24},{64,32},{72,40},{80,48},{88,56},{96,... | collective-permute-start | bytes 24584 | tf_op jit(solution)/shard_map/ppermute | solution.py:32
  245.1 18.4 %collective-permute-start.36 = (f32[2,4,256]{2,1,0:T(4,128)S(1)}, f32[2,4,256]{2,1,0:T(4,128)S(1)}, u32[]{:S(2)}, u32[]{:S(2)}) collective-permute-start(f32[2,4,256]{2,1,0:T(4,128)S(1)} %get-tuple-element.64), channel_id=1, source_target_pairs={{40,0},{48,8},{56,16},{64,24},{72,32},{80,40},{88,48},{96,56},{104... | collective-permute-start | bytes 24584 | tf_op jit(solution)/shard_map/ppermute | solution.py:32
  256.0 21.3 %collective-permute-start.37 = (f32[2,4,256]{2,1,0:T(4,128)S(1)}, f32[2,4,256]{2,1,0:T(4,128)S(1)}, u32[]{:S(2)}, u32[]{:S(2)}) collective-permute-start(f32[2,4,256]{2,1,0:T(4,128)S(1)} %get-tuple-element.64), channel_id=1, source_target_pairs={{48,0},{56,8},{64,16},{72,24},{80,32},{88,40},{96,48},{104,56},{11... | collective-permute-start | bytes 24584 | tf_op jit(solution)/shard_map/ppermute | solution.py:32
  257.9 24.9 %collective-permute-start.38 = (f32[2,4,256]{2,1,0:T(4,128)S(1)}, f32[2,4,256]{2,1,0:T(4,128)S(1)}, u32[]{:S(2)}, u32[]{:S(2)}) collective-permute-start(f32[2,4,256]{2,1,0:T(4,128)S(1)} %get-tuple-element.64), channel_id=1, source_target_pairs={{56,0},{64,8},{72,16},{80,24},{88,32},{96,40},{104,48},{112,56},{1... | collective-permute-start | bytes 24584 | tf_op jit(solution)/shard_map/ppermute | solution.py:32
  259.8 24.1 %collective-permute-start.39 = (f32[2,4,256]{2,1,0:T(4,128)S(1)}, f32[2,4,256]{2,1,0:T(4,128)S(1)}, u32[]{:S(2)}, u32[]{:S(2)}) collective-permute-start(f32[2,4,256]{2,1,0:T(4,128)S(1)} %get-tuple-element.64), channel_id=1, source_target_pairs={{64,0},{72,8},{80,16},{88,24},{96,32},{104,40},{112,48},{120,56},{... | collective-permute-start | bytes 24584 | tf_op jit(solution)/shard_map/ppermute | solution.py:32
  (39 other events, 539.4 us)

commit v2 on v1

--- a/solution.py
+++ b/solution.py
@@ -54,7 +54,6 @@
     span = (reach + 1) * rows
     scale = width ** (-0.5)
 
-    all_ids = lax.all_gather(doc_ids, "seq", axis=0, tiled=True)
     local = jnp.arange(rows, dtype=jnp.int32)
     positions = me * rows + local
     head_id = doc_ids[0]
@@ -67,6 +66,13 @@
     lq, lk, lv, ldo = shape3(light_q), shape3(light_k), shape3(light_v), shape3(light_grad_out)
     sq, sk, sv, sdo = shape3(soft_q), shape3(soft_k), shape3(soft_v), shape3(soft_grad_out)
     lqf, lkf, lvf, ldof = (a.astype(jnp.float32) for a in (lq, lk, lv, ldo))
+    cols = heads * width
+    id_cols = jnp.broadcast_to(doc_ids.astype(jnp.bfloat16)[:, None], (rows, 128))
+
+    own_kv = jnp.concatenate([soft_k, soft_v, id_cols], axis=1)
+    own_qg = jnp.concatenate([soft_q, soft_grad_out, id_cols], axis=1)
+    fwd = relay(own_kv, reach, 1)
+    bwd = relay(own_qg, reach, -1)
 
     since_start = (local + 1).astype(jnp.float32)
     until_end = (rows - 1 - local).astype(jnp.float32)
@@ -76,9 +82,35 @@
     head_part = start_decay * (doc_ids == head_id)[:, None]
     send_state = mixed("shk,shv->hkv", lkf * tail_part[:, :, None], lvf)
     back_state = mixed("thq,tho->hqo", lqf * head_part[:, :, None], ldof)
+    keep = jnp.exp(-slope * rows)
+    head_f = head_id.astype(jnp.float32)
+    tail_f = tail_id.astype(jnp.float32)
 
-    fwd = relay((jnp.concatenate([soft_k, soft_v], axis=1), send_state), reach, 1)
-    bwd = relay((jnp.concatenate([soft_q, soft_grad_out], axis=1), back_state), reach, -1)
+    def tagged(state, tag_a, tag_b):
+        tags = jnp.zeros((heads, 8, width), jnp.float32).at[:, 0, 0].set(tag_a).at[:, 0, 1].set(tag_b)
+        return jnp.concatenate([state, tags], axis=1)
+
+    def untag(message):
+        return message[:, :width], message[0, width, 0], message[0, width, 1]
+
+    got, src_head, src_tail = untag(shifted(tagged(send_state, head_f, tail_f), 1))
+    window = jnp.where((me >= 1) & (src_tail == head_f), 1.0, 0.0) * got
+    step = 1
+    while step < reach:
+        got, src_head, _ = untag(shifted(tagged(window, head_f, tail_f), step))
+        use = (me >= step) & (src_head == head_f)
+        window = window + jnp.where(use, keep ** step, 0.0)[:, None, None] * got
+        step *= 2
+    inherited = window
+    got, src_head, src_tail = untag(shifted(tagged(back_state, head_f, tail_f), -1))
+    window = jnp.where((me + 1 < count) & (src_head == tail_f), 1.0, 0.0) * got
+    step = 1
+    while step < reach:
+        got, _, src_tail = untag(shifted(tagged(window, head_f, tail_f), -step))
+        use = (me + step < count) & (src_tail == tail_f)
+        window = window + jnp.where(use, keep ** step, 0.0)[:, None, None] * got
+        step *= 2
+    ahead = window
 
     inside = (doc_ids[:, None] == doc_ids[None, :]) & (local[None, :] <= local[:, None])
     distance = jnp.maximum(local[:, None] - local[None, :], 0).astype(jnp.float32)
@@ -89,33 +121,16 @@
     light_dq = mixed("hts,shk->thk", grad_scores, lkf)
     light_dk = mixed("hts,thk->shk", grad_scores, lqf)
     light_dv = mixed("hts,thv->shv", scores, ldof)
-
-    keep = jnp.exp(-slope * rows)
-    inherited = jnp.zeros_like(send_state)
-    for k in range(1, reach + 1):
-        source = me - k
-        source_tail = all_ids[jnp.clip(source * rows + rows - 1, 0, total_rows - 1)]
-        use = (source >= 0) & (source_tail == head_id)
-        factor = jnp.where(use, keep ** (k - 1), 0.0)
-        inherited = inherited + factor[:, None, None] * fwd[k - 1][1]
-    ahead = jnp.zeros_like(back_state)
-    for k in range(1, reach + 1):
-        source = me + k
-        source_head = all_ids[jnp.clip(source * rows, 0, total_rows - 1)]
-        use = (source < count) & (source_head == tail_id)
-        factor = jnp.where(use, keep ** (k - 1), 0.0)
-        ahead = ahead + factor[:, None, None] * bwd[k - 1][1]
     light_out = light_out + mixed("thk,hkv->thv", lqf * head_part[:, :, None], inherited)
     light_dq = light_dq + mixed("thv,hkv->thk", ldof * head_part[:, :, None], inherited)
     light_dk = light_dk + mixed("hqo,sho->shq", ahead, lvf) * tail_part[:, :, None]
     light_dv = light_dv + mixed("hqo,shq->sho", ahead, lkf) * tail_part[:, :, None]
 
-    key_blocks = [jnp.concatenate([soft_k, soft_v], axis=1)] + [f[0] for f in fwd]
-    key_all = jnp.concatenate(key_blocks[::-1], axis=0)
-    keys = key_all[:, : heads * width].reshape(span, heads, width)
-    values = key_all[:, heads * width :].reshape(span, heads, width)
+    key_all = jnp.concatenate(([own_kv] + fwd)[::-1], axis=0)
+    keys = key_all[:, :cols].reshape(span, heads, width)
+    values = key_all[:, cols : 2 * cols].reshape(span, heads, width)
+    key_ids = key_all[:, 2 * cols].astype(jnp.int32)
     key_pos = (me - reach) * rows + jnp.arange(span, dtype=jnp.int32)
-    key_ids = all_ids[jnp.clip(key_pos, 0, total_rows - 1)]
     allowed = (
         (key_pos[None, :] >= 0)
         & (key_pos[None, :] <= positions[:, None])
@@ -137,14 +152,13 @@
 
     stats = jnp.stack([lse, delta])
     stat_blocks = [stats] + [shifted(stats, -k) for k in range(1, reach + 1)]
-    query_blocks = [jnp.concatenate([soft_q, soft_grad_out], axis=1)] + [b[0] for b in bwd]
-    query_all = jnp.concatenate(query_blocks, axis=0)
-    queries = query_all[:, : heads * width].reshape(span, heads, width)
-    grads = query_all[:, heads * width :].reshape(span, heads, width)
+    query_all = jnp.concatenate([own_qg] + bwd, axis=0)
+    queries = query_all[:, :cols].reshape(span, heads, width)
+    grads = query_all[:, cols : 2 * cols].reshape(span, heads, width)
+    query_ids = query_all[:, 2 * cols].astype(jnp.int32)
     stat_all = jnp.concatenate(stat_blocks, axis=2)
     lse_all, delta_all = stat_all[0], stat_all[1]
     query_pos = me * rows + jnp.arange(span, dtype=jnp.int32)
-    query_ids = all_ids[jnp.clip(query_pos, 0, total_rows - 1)]
     seen = (
         (query_pos[:, None] < total_rows)
         & (positions[None, :] <= query_pos[:, None])

time: 305 us -> 298 us (0.977)
  waiting for transfers between devices: 31.6 us -> 84.9 us
  local copies, waits for them, and re-layouts: 74.1 us -> 53.4 us
  blocking collectives: 20.6 us -> 0 us
  starting transfers between devices: 105 us -> 87.6 us
  between operations: 21.5 us -> 8.22 us
  other arithmetic: 14.8 us -> 22.3 us
  matrix products: 34.8 us -> 37.9 us
    ppermute x32 -> x16, starting transfers between devices: 94 us -> 50.7 us  [relay(): cur = lax.ppermute(cur, 'seq', pairs)]
    ppermute x32 -> x16, waiting for transfers between devices: 11.7 us -> 50.2 us  [relay(): cur = lax.ppermute(cur, 'seq', pairs)]
    ppermute x8 -> x16, starting transfers between devices: 11.1 us -> 37 us  [shifted(): return lax.ppermute(value, 'seq', pairs)]
    gather x2 -> x0, local copies, waits for them, and re-layouts: 24.6 us -> none  [the longest x1 12.3 us: per_device(): key_ids = all_ids[jnp.clip(key_pos, 0, total_rows - 1)]]
    all_gather x1 -> x0, blocking collectives: 20.6 us -> none  [per_device(): all_ids = lax.all_gather(doc_ids, 'seq', axis=0, tiled=True)]
    ppermute x8 -> x16, waiting for transfers between devices: 19.8 us -> 34.7 us  [shifted(): return lax.ppermute(value, 'seq', pairs)]
    slice x3 -> x11, local copies, waits for them, and re-layouts: 5.78 us -> 11.5 us  [the longest x8 7.22 us: untag(): return (message[:, :width], message[0, width, 0], message[0, width, 1])]
    dot_general x10, matrix products: 5.85 us -> 10.1 us  [mixed(): jnp.einsum(form, left, right, precision=PRECISE, preferred_element_type=j...]
  transfers between devices with their start and end apart: 40 -> 32, of which waited for: 9 -> 17; matrix products, arithmetic and copies ran while one was open for 32% -> 25% of each run, Pallas kernels for 0% -> 0%
where the time goes in v2:
time: 298 us; the launch traced here: 294 us
  starting transfers between devices  87.6 us (29%)
  waiting for transfers between devices  84.9 us (28%)
  local copies, waits for them, and re-layouts  53.4 us (18%)
  matrix products  37.9 us (13%)
  other arithmetic  22.3 us (7%)
  between operations  8.22 us (3%)
    ppermute x16, starting transfers between devices, relay(): cur = lax.ppermute(cur, 'seq', pairs)  50.7 us
    ppermute x16, waiting for transfers between devices, relay(): cur = lax.ppermute(cur, 'seq', pairs)  50.2 us
    ppermute x16, starting transfers between devices, shifted(): return lax.ppermute(value, 'seq', pairs)  37 us
    unnamed x97, local copies, waits for them, and re-layouts  36.4 us
    ppermute x16, waiting for transfers between devices, shifted(): return lax.ppermute(value, 'seq', pairs)  34.7 us
    dot_general x8, matrix products, exact(): return jnp.einsum(form, left, right, preferred_element_type=jnp.float32)  27.8 us
    dot_general x10, matrix products, mixed(): jnp.einsum(form, left, right, precision=PRECISE, preferred_element_type=j...  10.1 us
    slice x8, local copies, waits for them, and re-layouts, untag(): return (message[:, :width], message[0, width, 0], message[0, width, 1])  7.22 us
  transfers between devices with their start and end apart: 32, of which 17 were waited for; matrix products, arithmetic and copies ran while one was open for 25% of the time, Pallas kernels for 0%

profile of v2, /device:TPU:1, one launch (start us, length us, event | category | flops | bytes accessed | tf_op | source)
XLA Modules:
  0.0 294.3 jit_solution(5932898690042778423)
XLA Ops:
  10.9 8.7 %collective-permute-start.4 = (f32[4,136,128]{2,1,0:T(8,128)S(1)}, f32[4,136,128]{2,1,0:T(8,128)S(1)}, u32[]{:S(2)}, u32[]{:S(2)}) collective-permute-start(f32[4,136,128]{2,1,0:T(8,128)S(1)} %pad_maximum_fusion.3), channel_id=1, source_target_pairs={{8,0},{16,8},{24,16},{32,24},{40,32},{48,40},{56,48},{64,56},{72,6... | collective-permute-start | bytes 835592 | tf_op jit(solution)/shard_map/ppermute | solution.py:32
  26.6 3.6 %collective-permute-start.8 = (bf16[256,1152]{0,1:T(8,128)(2,1)}, bf16[256,1152]{0,1:T(8,128)(2,1)S(1)}, u32[]{:S(2)}, u32[]{:S(2)}) collective-permute-start(bf16[256,1152]{0,1:T(8,128)(2,1)} %pad_maximum_fusion.9), channel_id=1, source_target_pairs={{0,8},{8,16},{16,24},{24,32},{32,40},{40,48},{48,56},{56,64},{64,7... | collective-permute-start | bytes 1769480 | tf_op jit(solution)/shard_map/ppermute | solution.py:24
  39.6 4.0 %collective-permute-start.9 = (bf16[256,1152]{0,1:T(8,128)(2,1)S(1)}, bf16[256,1152]{0,1:T(8,128)(2,1)}, u32[]{:S(2)}, u32[]{:S(2)}) collective-permute-start(bf16[256,1152]{0,1:T(8,128)(2,1)S(1)} %collective-permute-done.8), channel_id=1, source_target_pairs={{0,8},{8,16},{16,24},{24,32},{32,40},{40,48},{48,56},{56,64},{64,7... | collective-permute-start | bytes 1769480 | tf_op jit(solution)/shard_map/ppermute | solution.py:24
  48.8 3.7 %collective-permute-start.1 = (f32[4,136,128]{2,1,0:T(8,128)S(1)}, f32[4,136,128]{2,1,0:T(8,128)S(1)}, u32[]{:S(2)}, u32[]{:S(2)}) collective-permute-start(f32[4,136,128]{2,1,0:T(8,128)S(1)} %get-tuple-element.170), channel_id=1, source_target_pairs={{0,8},{8,16},{16,24},{24,32},{32,40},{40,48},{48,56},{56,64},{64,7... | collective-permute-start | bytes 835592 | tf_op jit(solution)/shard_map/ppermute | solution.py:32
  57.9 4.4 %collective-permute-start.10 = (bf16[256,1152]{0,1:T(8,128)(2,1)}, bf16[256,1152]{0,1:T(8,128)(2,1)}, u32[]{:S(2)}, u32[]{:S(2)}) collective-permute-start(bf16[256,1152]{0,1:T(8,128)(2,1)} %collective-permute-done.9), channel_id=1, source_target_pairs={{0,8},{8,16},{16,24},{24,32},{32,40},{40,48},{48,56},{56,64},{64,7... | collective-permute-start | bytes 1769480 | tf_op jit(solution)/shard_map/ppermute | solution.py:24
  68.9 3.5 %collective-permute-done.10 = bf16[256,1152]{0,1:T(8,128)(2,1)} collective-permute-done((bf16[256,1152]{0,1:T(8,128)(2,1)}, bf16[256,1152]{0,1:T(8,128)(2,1)}, u32[]{:S(2)}, u32[]{:S(2)}) %collective-permute-start.10) | collective-permute-done | bytes 589856 | tf_op jit(solution)/shard_map/ppermute | solution.py:24
  72.4 4.4 %collective-permute-start.11 = (bf16[256,1152]{0,1:T(8,128)(2,1)}, bf16[256,1152]{0,1:T(8,128)(2,1)}, u32[]{:S(2)}, u32[]{:S(2)}) collective-permute-start(bf16[256,1152]{0,1:T(8,128)(2,1)} %collective-permute-done.10), channel_id=1, source_target_pairs={{0,8},{8,16},{16,24},{24,32},{32,40},{40,48},{48,56},{56,64},{64,7... | collective-permute-start | bytes 1769480 | tf_op jit(solution)/shard_map/ppermute | solution.py:24
  83.9 4.4 %collective-permute-start.12 = (bf16[256,1152]{0,1:T(8,128)(2,1)}, bf16[256,1152]{0,1:T(8,128)(2,1)S(1)}, u32[]{:S(2)}, u32[]{:S(2)}) collective-permute-start(bf16[256,1152]{0,1:T(8,128)(2,1)} %collective-permute-done.11), channel_id=1, source_target_pairs={{0,8},{8,16},{16,24},{24,32},{32,40},{40,48},{48,56},{56,64},{64,7... | collective-permute-start | bytes 1769480 | tf_op jit(solution)/shard_map/ppermute | solution.py:24
  91.0 4.4 %collective-permute-done.12 = bf16[256,1152]{0,1:T(8,128)(2,1)S(1)} collective-permute-done((bf16[256,1152]{0,1:T(8,128)(2,1)}, bf16[256,1152]{0,1:T(8,128)(2,1)S(1)}, u32[]{:S(2)}, u32[]{:S(2)}) %collective-permute-start.12) | collective-permute-done | bytes 589856 | tf_op jit(solution)/shard_map/ppermute | solution.py:24
  95.4 4.3 %collective-permute-start.13 = (bf16[256,1152]{0,1:T(8,128)(2,1)S(1)}, bf16[256,1152]{0,1:T(8,128)(2,1)}, u32[]{:S(2)}, u32[]{:S(2)}) collective-permute-start(bf16[256,1152]{0,1:T(8,128)(2,1)S(1)} %collective-permute-done.12), channel_id=1, source_target_pairs={{0,8},{8,16},{16,24},{24,32},{32,40},{40,48},{48,56},{56,64},{64,7... | collective-permute-start | bytes 1769480 | tf_op jit(solution)/shard_map/ppermute | solution.py:24
  100.4 4.0 %collective-permute-start.3 = (f32[4,136,128]{2,1,0:T(8,128)}, f32[4,136,128]{2,1,0:T(8,128)}, u32[]{:S(2)}, u32[]{:S(2)}) collective-permute-start(f32[4,136,128]{2,1,0:T(8,128)} %pad_maximum_fusion.4), channel_id=1, source_target_pairs={{0,32},{8,40},{16,48},{24,56},{32,64},{40,72},{48,80},{56,88},{64,... | collective-permute-start | bytes 835592 | tf_op jit(solution)/shard_map/ppermute | solution.py:32
  105.2 4.3 %collective-permute-done.13 = bf16[256,1152]{0,1:T(8,128)(2,1)} collective-permute-done((bf16[256,1152]{0,1:T(8,128)(2,1)S(1)}, bf16[256,1152]{0,1:T(8,128)(2,1)}, u32[]{:S(2)}, u32[]{:S(2)}) %collective-permute-start.13) | collective-permute-done | bytes 589856 | tf_op jit(solution)/shard_map/ppermute | solution.py:24
  109.5 4.6 %collective-permute-start.14 = (bf16[256,1152]{0,1:T(8,128)(2,1)}, bf16[256,1152]{0,1:T(8,128)(2,1)}, u32[]{:S(2)}, u32[]{:S(2)}) collective-permute-start(bf16[256,1152]{0,1:T(8,128)(2,1)} %collective-permute-done.13), channel_id=1, source_target_pairs={{0,8},{8,16},{16,24},{24,32},{32,40},{40,48},{48,56},{56,64},{64,7... | collective-permute-start | bytes 1769480 | tf_op jit(solution)/shard_map/ppermute | solution.py:24
  124.1 5.2 %collective-permute-start.15 = (bf16[256,1152]{0,1:T(8,128)(2,1)}, bf16[256,1152]{0,1:T(8,128)(2,1)}, u32[]{:S(2)}, u32[]{:S(2)}) collective-permute-start(bf16[256,1152]{0,1:T(8,128)(2,1)} %collective-permute-done.14), channel_id=1, source_target_pairs={{0,8},{8,16},{16,24},{24,32},{32,40},{40,48},{48,56},{56,64},{64,7... | collective-permute-start | bytes 1769480 | tf_op jit(solution)/shard_map/ppermute | solution.py:24
  150.6 5.9 %collective-permute-done.16 = bf16[256,1152]{0,1:T(8,128)(2,1)S(1)} collective-permute-done((bf16[256,1152]{0,1:T(8,128)(2,1)S(1)}, bf16[256,1152]{0,1:T(8,128)(2,1)S(1)}, u32[]{:S(2)}, u32[]{:S(2)}) %collective-permute-start.16) | collective-permute-done | bytes 589856 | tf_op jit(solution)/shard_map/ppermute | solution.py:24
  160.9 6.8 %collective-permute-done.17 = bf16[256,1152]{0,1:T(8,128)(2,1)S(1)} collective-permute-done((bf16[256,1152]{0,1:T(8,128)(2,1)S(1)}, bf16[256,1152]{0,1:T(8,128)(2,1)S(1)}, u32[]{:S(2)}, u32[]{:S(2)}) %collective-permute-start.17) | collective-permute-done | bytes 589856 | tf_op jit(solution)/shard_map/ppermute | solution.py:24
  169.6 4.4 %multiply_reduce_fusion = (f32[256,4]{0,1:T(4,128)S(1)}, bf16[256,4,128]{0,2,1:T(8,128)(2,1)}) fusion(bf16[256,512]{0,1:T(8,128)(2,1)S(1)} %copy-done.12, f32[256,4]{0,1:T(4,128)S(1)} %bitcast.222, bf16[2304,4,128]{0,2,1:T(8,128)(2,1)S(1)} %bitcast.211, f32[4,2304,256]{2,1,0:T(8,128)S(1)} %get-tuple-element.187, f32[4,256]{1,0:T(4,128)S(1)} %get-tuple-element.186, ...), kind=kOutput, calls=%fused_computation.60 | convolution fusion | flops 616561664 | bytes 12922880 | tf_op jit(solution)/shard_map/hts,shd->htd/dot_general | solution.py:15
  181.8 9.3 %fusion.33 = bf16[4,128,256]{2,1,0:T(8,128)(2,1)} fusion(bf16[2304,4,128]{0,2,1:T(8,128)(2,1)S(1)} %bitcast.195, f32[4,2304,256]{2,1,0:T(8,128)} %copy-done.2, bf16[2304,4,128]{0,2,1:T(8,128)(2,1)} %bitcast.212, bf16[256,4,128]{0,2,1:T(8,128)(2,1)} %bitcast.219, f32[4,256]{1,0:T(4,128)S(1)} %bitcast.225, f32[4,256]{1,0:T(4,128)S(1)} %log_add_fusion, ...), kind=kOutput, calls=%fused_computation.46 | convolution fusion | flops 1224736768 | bytes 15278080 | tf_op jit(solution)/shard_map/hts,shd->thd/dot_general | solution.py:15
  200.8 11.6 %collective-permute-done.26 = f32[2,4,256]{2,1,0:T(4,128)S(1)} collective-permute-done((f32[2,4,256]{2,1,0:T(4,128)S(1)}, f32[2,4,256]{2,1,0:T(4,128)S(1)}, u32[]{:S(2)}, u32[]{:S(2)}) %collective-permute-start.26) | collective-permute-done | bytes 8224 | tf_op jit(solution)/shard_map/ppermute | solution.py:32
  215.6 10.0 %collective-permute-done.27 = f32[2,4,256]{2,1,0:T(4,128)S(1)} collective-permute-done((f32[2,4,256]{2,1,0:T(4,128)S(1)}, f32[2,4,256]{2,1,0:T(4,128)S(1)}, u32[]{:S(2)}, u32[]{:S(2)}) %collective-permute-start.27) | collective-permute-done | bytes 8224 | tf_op jit(solution)/shard_map/ppermute | solution.py:32
  226.9 6.9 %collective-permute-done.31 = f32[2,4,256]{2,1,0:T(4,128)S(1)} collective-permute-done((f32[2,4,256]{2,1,0:T(4,128)S(1)}, f32[2,4,256]{2,1,0:T(4,128)S(1)}, u32[]{:S(2)}, u32[]{:S(2)}) %collective-permute-start.31) | collective-permute-done | bytes 8224 | tf_op jit(solution)/shard_map/ppermute | solution.py:32
  237.9 11.6 %collective-permute-done.21 = bf16[256,1152]{0,1:T(8,128)(2,1)S(1)} collective-permute-done((bf16[256,1152]{0,1:T(8,128)(2,1)S(1)}, bf16[256,1152]{0,1:T(8,128)(2,1)S(1)}, u32[]{:S(2)}, u32[]{:S(2)}) %collective-permute-start.21) | collective-permute-done | bytes 589856 | tf_op jit(solution)/shard_map/ppermute | solution.py:24
  265.6 6.3 %collective-permute-done.23 = bf16[256,1152]{0,1:T(8,128)(2,1)S(1)} collective-permute-done((bf16[256,1152]{0,1:T(8,128)(2,1)S(1)}, bf16[256,1152]{0,1:T(8,128)(2,1)S(1)}, u32[]{:S(2)}, u32[]{:S(2)}) %collective-permute-start.23) | collective-permute-done | bytes 589856 | tf_op jit(solution)/shard_map/ppermute | solution.py:24
  286.5 7.0 %fusion.29 = bf16[4,128,256]{2,1,0:T(8,128)(2,1)S(1)} fusion(bf16[2304,4,128]{0,2,1:T(8,128)(2,1)} %bitcast.197, f32[4,2304,256]{2,1,0:T(8,128)} %copy-done.3, bf16[2304,4,128]{0,2,1:T(8,128)(2,1)S(1)} %bitcast.193, bf16[256,4,128]{0,2,1:T(8,128)(2,1)S(1)} %bitcast.210, f32[4,2304]{1,0:T(4,128)S(1)} %get-tuple-element.166), kind=kOutput, calls=%fused_computation.44 | convolution fusion | flops 1215299584 | bytes 14716928 | tf_op jit(solution)/shard_map/hts,thd->shd/dot_general | solution.py:15
  (215 shorter events, 142.8 us)
Async XLA Ops:
  10.9 11.7 %collective-permute-start.4 = (f32[4,136,128]{2,1,0:T(8,128)S(1)}, f32[4,136,128]{2,1,0:T(8,128)S(1)}, u32[]{:S(2)}, u32[]{:S(2)}) collective-permute-start(f32[4,136,128]{2,1,0:T(8,128)S(1)} %pad_maximum_fusion.3), channel_id=1, source_target_pairs={{8,0},{16,8},{24,16},{32,24},{40,32},{48,40},{56,48},{64,56},{72,6... | collective-permute-start | bytes 835592 | tf_op jit(solution)/shard_map/ppermute | solution.py:32
  26.6 13.0 %collective-permute-start.8 = (bf16[256,1152]{0,1:T(8,128)(2,1)}, bf16[256,1152]{0,1:T(8,128)(2,1)S(1)}, u32[]{:S(2)}, u32[]{:S(2)}) collective-permute-start(bf16[256,1152]{0,1:T(8,128)(2,1)} %pad_maximum_fusion.9), channel_id=1, source_target_pairs={{0,8},{8,16},{16,24},{24,32},{32,40},{40,48},{48,56},{56,64},{64,7... | collective-permute-start | bytes 1769480 | tf_op jit(solution)/shard_map/ppermute | solution.py:24
  39.6 18.3 %collective-permute-start.9 = (bf16[256,1152]{0,1:T(8,128)(2,1)S(1)}, bf16[256,1152]{0,1:T(8,128)(2,1)}, u32[]{:S(2)}, u32[]{:S(2)}) collective-permute-start(bf16[256,1152]{0,1:T(8,128)(2,1)S(1)} %collective-permute-done.8), channel_id=1, source_target_pairs={{0,8},{8,16},{16,24},{24,32},{32,40},{40,48},{48,56},{56,64},{64,7... | collective-permute-start | bytes 1769480 | tf_op jit(solution)/shard_map/ppermute | solution.py:24
  53.3 24.1 %collective-permute-start.7 = (f32[4,136,128]{2,1,0:T(8,128)}, f32[4,136,128]{2,1,0:T(8,128)S(1)}, u32[]{:S(2)}, u32[]{:S(2)}) collective-permute-start(f32[4,136,128]{2,1,0:T(8,128)} %get-tuple-element.169), channel_id=1, source_target_pairs={{32,0},{40,8},{48,16},{56,24},{64,32},{72,40},{80,48},{88,56},{96,... | collective-permute-start | bytes 835592 | tf_op jit(solution)/shard_map/ppermute | solution.py:32
  57.9 14.5 %collective-permute-start.10 = (bf16[256,1152]{0,1:T(8,128)(2,1)}, bf16[256,1152]{0,1:T(8,128)(2,1)}, u32[]{:S(2)}, u32[]{:S(2)}) collective-permute-start(bf16[256,1152]{0,1:T(8,128)(2,1)} %collective-permute-done.9), channel_id=1, source_target_pairs={{0,8},{8,16},{16,24},{24,32},{32,40},{40,48},{48,56},{56,64},{64,7... | collective-permute-start | bytes 1769480 | tf_op jit(solution)/shard_map/ppermute | solution.py:24
  63.4 15.2 %collective-permute-start.2 = (f32[4,136,128]{2,1,0:T(8,128)S(1)}, f32[4,136,128]{2,1,0:T(8,128)}, u32[]{:S(2)}, u32[]{:S(2)}) collective-permute-start(f32[4,136,128]{2,1,0:T(8,128)S(1)} %pad_maximum_fusion.5), channel_id=1, source_target_pairs={{0,16},{8,24},{16,32},{24,40},{32,48},{40,56},{48,64},{56,72},{64,... | collective-permute-start | bytes 835592 | tf_op jit(solution)/shard_map/ppermute | solution.py:32
  72.4 11.5 %collective-permute-start.11 = (bf16[256,1152]{0,1:T(8,128)(2,1)}, bf16[256,1152]{0,1:T(8,128)(2,1)}, u32[]{:S(2)}, u32[]{:S(2)}) collective-permute-start(bf16[256,1152]{0,1:T(8,128)(2,1)} %collective-permute-done.10), channel_id=1, source_target_pairs={{0,8},{8,16},{16,24},{24,32},{32,40},{40,48},{48,56},{56,64},{64,7... | collective-permute-start | bytes 1769480 | tf_op jit(solution)/shard_map/ppermute | solution.py:24
  83.9 11.5 %collective-permute-start.12 = (bf16[256,1152]{0,1:T(8,128)(2,1)}, bf16[256,1152]{0,1:T(8,128)(2,1)S(1)}, u32[]{:S(2)}, u32[]{:S(2)}) collective-permute-start(bf16[256,1152]{0,1:T(8,128)(2,1)} %collective-permute-done.11), channel_id=1, source_target_pairs={{0,8},{8,16},{16,24},{24,32},{32,40},{40,48},{48,56},{56,64},{64,7... | collective-permute-start | bytes 1769480 | tf_op jit(solution)/shard_map/ppermute | solution.py:24
  95.4 14.1 %collective-permute-start.13 = (bf16[256,1152]{0,1:T(8,128)(2,1)S(1)}, bf16[256,1152]{0,1:T(8,128)(2,1)}, u32[]{:S(2)}, u32[]{:S(2)}) collective-permute-start(bf16[256,1152]{0,1:T(8,128)(2,1)S(1)} %collective-permute-done.12), channel_id=1, source_target_pairs={{0,8},{8,16},{16,24},{24,32},{32,40},{40,48},{48,56},{56,64},{64,7... | collective-permute-start | bytes 1769480 | tf_op jit(solution)/shard_map/ppermute | solution.py:24
  100.4 21.7 %collective-permute-start.3 = (f32[4,136,128]{2,1,0:T(8,128)}, f32[4,136,128]{2,1,0:T(8,128)}, u32[]{:S(2)}, u32[]{:S(2)}) collective-permute-start(f32[4,136,128]{2,1,0:T(8,128)} %pad_maximum_fusion.4), channel_id=1, source_target_pairs={{0,32},{8,40},{16,48},{24,56},{32,64},{40,72},{48,80},{56,88},{64,... | collective-permute-start | bytes 835592 | tf_op jit(solution)/shard_map/ppermute | solution.py:32
  109.5 14.6 %collective-permute-start.14 = (bf16[256,1152]{0,1:T(8,128)(2,1)}, bf16[256,1152]{0,1:T(8,128)(2,1)}, u32[]{:S(2)}, u32[]{:S(2)}) collective-permute-start(bf16[256,1152]{0,1:T(8,128)(2,1)} %collective-permute-done.13), channel_id=1, source_target_pairs={{0,8},{8,16},{16,24},{24,32},{32,40},{40,48},{48,56},{56,64},{64,7... | collective-permute-start | bytes 1769480 | tf_op jit(solution)/shard_map/ppermute | solution.py:24
  124.1 12.3 %collective-permute-start.15 = (bf16[256,1152]{0,1:T(8,128)(2,1)}, bf16[256,1152]{0,1:T(8,128)(2,1)}, u32[]{:S(2)}, u32[]{:S(2)}) collective-permute-start(bf16[256,1152]{0,1:T(8,128)(2,1)} %collective-permute-done.14), channel_id=1, source_target_pairs={{0,8},{8,16},{16,24},{24,32},{32,40},{40,48},{48,56},{56,64},{64,7... | collective-permute-start | bytes 1769480 | tf_op jit(solution)/shard_map/ppermute | solution.py:24
  144.6 11.9 %collective-permute-start.16 = (bf16[256,1152]{0,1:T(8,128)(2,1)S(1)}, bf16[256,1152]{0,1:T(8,128)(2,1)S(1)}, u32[]{:S(2)}, u32[]{:S(2)}) collective-permute-start(bf16[256,1152]{0,1:T(8,128)(2,1)S(1)} %get-tuple-element.164), channel_id=1, source_target_pairs={{8,0},{16,8},{24,16},{32,24},{40,32},{48,40},{56,48},{64,56},{72,6... | collective-permute-start | bytes 1769480 | tf_op jit(solution)/shard_map/ppermute | solution.py:24
  156.5 11.2 %collective-permute-start.17 = (bf16[256,1152]{0,1:T(8,128)(2,1)S(1)}, bf16[256,1152]{0,1:T(8,128)(2,1)S(1)}, u32[]{:S(2)}, u32[]{:S(2)}) collective-permute-start(bf16[256,1152]{0,1:T(8,128)(2,1)S(1)} %collective-permute-done.16), channel_id=1, source_target_pairs={{8,0},{16,8},{24,16},{32,24},{40,32},{48,40},{56,48},{64,56},{72,6... | collective-permute-start | bytes 1769480 | tf_op jit(solution)/shard_map/ppermute | solution.py:24
  167.7 12.2 %collective-permute-start.18 = (bf16[256,1152]{0,1:T(8,128)(2,1)S(1)}, bf16[256,1152]{0,1:T(8,128)(2,1)}, u32[]{:S(2)}, u32[]{:S(2)}) collective-permute-start(bf16[256,1152]{0,1:T(8,128)(2,1)S(1)} %collective-permute-done.17), channel_id=1, source_target_pairs={{8,0},{16,8},{24,16},{32,24},{40,32},{48,40},{56,48},{64,56},{72,6... | collective-permute-start | bytes 1769480 | tf_op jit(solution)/shard_map/ppermute | solution.py:24
  174.0 52.9 %collective-permute-start.30 = (f32[2,4,256]{2,1,0:T(4,128)S(1)}, f32[2,4,256]{2,1,0:T(4,128)S(1)}, u32[]{:S(2)}, u32[]{:S(2)}) collective-permute-start(f32[2,4,256]{2,1,0:T(4,128)S(1)} %get-tuple-element.173), channel_id=1, source_target_pairs={{56,0},{64,8},{72,16},{80,24},{88,32},{96,40},{104,48},{112,56},{1... | collective-permute-start | bytes 24584 | tf_op jit(solution)/shard_map/ppermute | solution.py:32
  175.3 51.6 %collective-permute-start.29 = (f32[2,4,256]{2,1,0:T(4,128)S(1)}, f32[2,4,256]{2,1,0:T(4,128)S(1)}, u32[]{:S(2)}, u32[]{:S(2)}) collective-permute-start(f32[2,4,256]{2,1,0:T(4,128)S(1)} %get-tuple-element.173), channel_id=1, source_target_pairs={{48,0},{56,8},{64,16},{72,24},{80,32},{88,40},{96,48},{104,56},{11... | collective-permute-start | bytes 24584 | tf_op jit(solution)/shard_map/ppermute | solution.py:32
  176.6 50.2 %collective-permute-start.28 = (f32[2,4,256]{2,1,0:T(4,128)S(1)}, f32[2,4,256]{2,1,0:T(4,128)S(1)}, u32[]{:S(2)}, u32[]{:S(2)}) collective-permute-start(f32[2,4,256]{2,1,0:T(4,128)S(1)} %get-tuple-element.173), channel_id=1, source_target_pairs={{40,0},{48,8},{56,16},{64,24},{72,32},{80,40},{88,48},{96,56},{104... | collective-permute-start | bytes 24584 | tf_op jit(solution)/shard_map/ppermute | solution.py:32
  177.9 16.8 %collective-permute-start.24 = (f32[2,4,256]{2,1,0:T(4,128)S(1)}, f32[2,4,256]{2,1,0:T(4,128)S(1)}, u32[]{:S(2)}, u32[]{:S(2)}) collective-permute-start(f32[2,4,256]{2,1,0:T(4,128)S(1)} %get-tuple-element.173), channel_id=1, source_target_pairs={{8,0},{16,8},{24,16},{32,24},{40,32},{48,40},{56,48},{64,56},{72,6... | collective-permute-start | bytes 24584 | tf_op jit(solution)/shard_map/ppermute | solution.py:32
  179.9 33.8 %collective-permute-start.19 = (bf16[256,1152]{0,1:T(8,128)(2,1)}, bf16[256,1152]{0,1:T(8,128)(2,1)}, u32[]{:S(2)}, u32[]{:S(2)}) collective-permute-start(bf16[256,1152]{0,1:T(8,128)(2,1)} %collective-permute-done.18), channel_id=1, source_target_pairs={{8,0},{16,8},{24,16},{32,24},{40,32},{48,40},{56,48},{64,56},{72,6... | collective-permute-start | bytes 1769480 | tf_op jit(solution)/shard_map/ppermute | solution.py:24
  199.5 12.9 %collective-permute-start.26 = (f32[2,4,256]{2,1,0:T(4,128)S(1)}, f32[2,4,256]{2,1,0:T(4,128)S(1)}, u32[]{:S(2)}, u32[]{:S(2)}) collective-permute-start(f32[2,4,256]{2,1,0:T(4,128)S(1)} %get-tuple-element.173), channel_id=1, source_target_pairs={{24,0},{32,8},{40,16},{48,24},{56,32},{64,40},{72,48},{80,56},{88,... | collective-permute-start | bytes 24584 | tf_op jit(solution)/shard_map/ppermute | solution.py:32
  212.3 13.2 %collective-permute-start.27 = (f32[2,4,256]{2,1,0:T(4,128)S(1)}, f32[2,4,256]{2,1,0:T(4,128)S(1)}, u32[]{:S(2)}, u32[]{:S(2)}) collective-permute-start(f32[2,4,256]{2,1,0:T(4,128)S(1)} %get-tuple-element.173), channel_id=1, source_target_pairs={{32,0},{40,8},{48,16},{56,24},{64,32},{72,40},{80,48},{88,56},{96,... | collective-permute-start | bytes 24584 | tf_op jit(solution)/shard_map/ppermute | solution.py:32
  213.6 20.2 %collective-permute-start.20 = (bf16[256,1152]{0,1:T(8,128)(2,1)}, bf16[256,1152]{0,1:T(8,128)(2,1)S(1)}, u32[]{:S(2)}, u32[]{:S(2)}) collective-permute-start(bf16[256,1152]{0,1:T(8,128)(2,1)} %collective-permute-done.19), channel_id=1, source_target_pairs={{8,0},{16,8},{24,16},{32,24},{40,32},{48,40},{56,48},{64,56},{72,6... | collective-permute-start | bytes 1769480 | tf_op jit(solution)/shard_map/ppermute | solution.py:24
  233.9 15.6 %collective-permute-start.21 = (bf16[256,1152]{0,1:T(8,128)(2,1)S(1)}, bf16[256,1152]{0,1:T(8,128)(2,1)S(1)}, u32[]{:S(2)}, u32[]{:S(2)}) collective-permute-start(bf16[256,1152]{0,1:T(8,128)(2,1)S(1)} %collective-permute-done.20), channel_id=1, source_target_pairs={{8,0},{16,8},{24,16},{32,24},{40,32},{48,40},{56,48},{64,56},{72,6... | collective-permute-start | bytes 1769480 | tf_op jit(solution)/shard_map/ppermute | solution.py:24
  (39 other events, 580.9 us)

commit v3 on v2

--- a/solution.py
+++ b/solution.py
@@ -29,6 +29,17 @@
 def shifted(value, shift):
     count = lax.axis_size("seq")
     pairs = [(s, s + shift) for s in range(count) if 0 <= s + shift < count]
+    return lax.ppermute(value, "seq", pairs)
+
+
+def swapped(value):
+    count = lax.axis_size("seq")
+    return lax.ppermute(value, "seq", [(s, s ^ 1) for s in range(count)])
+
+
+def crossed(value, shift):
+    count = lax.axis_size("seq")
+    pairs = [(s, (s + shift) ^ 1) for s in range(count) if 0 <= s + shift < count]
     return lax.ppermute(value, "seq", pairs)
 
 
@@ -51,7 +62,6 @@
     me = lax.axis_index("seq")
     total_rows = rows * count
     reach = min(REACH, count - 1)
-    span = (reach + 1) * rows
     scale = width ** (-0.5)
 
     local = jnp.arange(rows, dtype=jnp.int32)
@@ -71,8 +81,7 @@
 
     own_kv = jnp.concatenate([soft_k, soft_v, id_cols], axis=1)
     own_qg = jnp.concatenate([soft_q, soft_grad_out, id_cols], axis=1)
-    fwd = relay(own_kv, reach, 1)
-    bwd = relay(own_qg, reach, -1)
+    partner = me ^ 1
 
     since_start = (local + 1).astype(jnp.float32)
     until_end = (rows - 1 - local).astype(jnp.float32)
@@ -93,24 +102,50 @@
     def untag(message):
         return message[:, :width], message[0, width, 0], message[0, width, 1]
 
-    got, src_head, src_tail = untag(shifted(tagged(send_state, head_f, tail_f), 1))
-    window = jnp.where((me >= 1) & (src_tail == head_f), 1.0, 0.0) * got
-    step = 1
-    while step < reach:
-        got, src_head, _ = untag(shifted(tagged(window, head_f, tail_f), step))
-        use = (me >= step) & (src_head == head_f)
-        window = window + jnp.where(use, keep ** step, 0.0)[:, None, None] * got
-        step *= 2
-    inherited = window
-    got, src_head, src_tail = untag(shifted(tagged(back_state, head_f, tail_f), -1))
-    window = jnp.where((me + 1 < count) & (src_head == tail_f), 1.0, 0.0) * got
-    step = 1
-    while step < reach:
-        got, _, src_tail = untag(shifted(tagged(window, head_f, tail_f), -step))
-        use = (me + step < count) & (src_tail == tail_f)
-        window = window + jnp.where(use, keep ** step, 0.0)[:, None, None] * got
-        step *= 2
-    ahead = window
+    chip_hops = (reach + 1) // 2
+    key_blocks = [(own_kv, me)]
+    query_blocks = [(own_qg, me)]
+    z_kv, z_qg = own_kv, own_qg
+    fwin = bwin = None
+    light_steps = [1]
+    while light_steps[-1] * 2 < reach:
+        light_steps.append(light_steps[-1] * 2)
+    for rnd in range(chip_hops + 1):
+        sent = {}
+        if rnd < chip_hops:
+            sent["z_kv"] = shifted(z_kv, 2)
+            sent["z_qg"] = shifted(z_qg, -2)
+        sent["w_kv"] = swapped(z_kv)
+        sent["w_qg"] = swapped(z_qg)
+        if rnd == 0:
+            sent["f"] = shifted(tagged(send_state, head_f, tail_f), 1)
+            sent["b"] = shifted(tagged(back_state, head_f, tail_f), -1)
+        elif rnd <= len(light_steps):
+            step = light_steps[rnd - 1]
+            sent["f"] = shifted(tagged(fwin, head_f, tail_f), step)
+            sent["b"] = shifted(tagged(bwin, head_f, tail_f), -step)
+        sent = lax.optimization_barrier(sent)
+        key_blocks.append((sent["w_kv"], partner - 2 * rnd))
+        query_blocks.append((sent["w_qg"], partner + 2 * rnd))
+        if rnd < chip_hops:
+            z_kv, z_qg = sent["z_kv"], sent["z_qg"]
+            key_blocks.append((z_kv, me - 2 * (rnd + 1)))
+            query_blocks.append((z_qg, me + 2 * (rnd + 1)))
+        if rnd == 0:
+            got, _, src_tail = untag(sent["f"])
+            fwin = jnp.where((me >= 1) & (src_tail == head_f), 1.0, 0.0) * got
+            got, src_head, _ = untag(sent["b"])
+            bwin = jnp.where((me + 1 < count) & (src_head == tail_f), 1.0, 0.0) * got
+        elif rnd <= len(light_steps):
+            step = light_steps[rnd - 1]
+            got, src_head, _ = untag(sent["f"])
+            use = (me >= step) & (src_head == head_f)
+            fwin = fwin + jnp.where(use, keep ** step, 0.0)[:, None, None] * got
+            got, _, src_tail = untag(sent["b"])
+            use = (me + step < count) & (src_tail == tail_f)
+            bwin = bwin + jnp.where(use, keep ** step, 0.0)[:, None, None] * got
+    inherited = fwin
+    ahead = bwin
 
     inside = (doc_ids[:, None] == doc_ids[None, :]) & (local[None, :] <= local[:, None])
     distance = jnp.maximum(local[:, None] - local[None, :], 0).astype(jnp.float32)
@@ -126,11 +161,12 @@
     light_dk = light_dk + mixed("hqo,sho->shq", ahead, lvf) * tail_part[:, :, None]
     light_dv = light_dv + mixed("hqo,shq->sho", ahead, lkf) * tail_part[:, :, None]
 
-    key_all = jnp.concatenate(([own_kv] + fwd)[::-1], axis=0)
+    span = len(key_blocks) * rows
+    key_all = jnp.concatenate([b for b, _ in key_blocks], axis=0)
     keys = key_all[:, :cols].reshape(span, heads, width)
     values = key_all[:, cols : 2 * cols].reshape(span, heads, width)
     key_ids = key_all[:, 2 * cols].astype(jnp.int32)
-    key_pos = (me - reach) * rows + jnp.arange(span, dtype=jnp.int32)
+    key_pos = jnp.concatenate([base * rows + local for _, base in key_blocks])
     allowed = (
         (key_pos[None, :] >= 0)
         & (key_pos[None, :] <= positions[:, None])
@@ -151,14 +187,17 @@
     soft_dq = exact("hts,shd->thd", dlogit, keys) * scale
 
     stats = jnp.stack([lse, delta])
-    stat_blocks = [stats] + [shifted(stats, -k) for k in range(1, reach + 1)]
-    query_all = jnp.concatenate([own_qg] + bwd, axis=0)
+    stat_blocks = [stats, swapped(stats)]
+    for rnd in range(1, chip_hops + 1):
+        stat_blocks.append(shifted(stats, -2 * rnd))
+        stat_blocks.append(crossed(stats, -2 * rnd))
+    query_all = jnp.concatenate([b for b, _ in query_blocks], axis=0)
     queries = query_all[:, :cols].reshape(span, heads, width)
     grads = query_all[:, cols : 2 * cols].reshape(span, heads, width)
     query_ids = query_all[:, 2 * cols].astype(jnp.int32)
     stat_all = jnp.concatenate(stat_blocks, axis=2)
     lse_all, delta_all = stat_all[0], stat_all[1]
-    query_pos = me * rows + jnp.arange(span, dtype=jnp.int32)
+    query_pos = jnp.concatenate([base * rows + local for _, base in query_blocks])
     seen = (
         (query_pos[:, None] < total_rows)
         & (positions[None, :] <= query_pos[:, None])

time: 298 us -> 299 us (level)
  waiting for transfers between devices: 84.9 us -> 67.9 us
  matrix products: 37.9 us -> 47 us
  local copies, waits for them, and re-layouts: 53.4 us -> 62.3 us
    ppermute x16 -> x15, waiting for transfers between devices: 50.2 us -> 5.59 us  [the longest x4 5.56 us: crossed(): return lax.ppermute(value, 'seq', pairs)]
    ppermute x16 -> x20, waiting for transfers between devices: 34.7 us -> 62.4 us  [shifted(): return lax.ppermute(value, 'seq', pairs)]
    dot_general x8, matrix products: 27.8 us -> 42.4 us  [exact(): return jnp.einsum(form, left, right, preferred_element_type=jnp.float32)]
    ppermute x16 -> x15, starting transfers between devices: 50.7 us -> 39 us  [the longest x11 33.4 us: swapped(): return lax.ppermute(value, 'seq', [(s, s ^ 1) for s in range(count)])]
    unnamed x97 -> x101, local copies, waits for them, and re-layouts: 36.4 us -> 47.2 us
    ppermute x16 -> x20, starting transfers between devices: 37 us -> 47.2 us  [shifted(): return lax.ppermute(value, 'seq', pairs)]
    dot_general x10, matrix products: 10.1 us -> 4.57 us  [mixed(): jnp.einsum(form, left, right, precision=PRECISE, preferred_element_type=j...]
  transfers between devices with their start and end apart: 32 -> 35, of which waited for: 17 -> 11; matrix products, arithmetic and copies ran while one was open for 25% -> 27% of each run, Pallas kernels for 0% -> 0%
where the time goes in v3:
time: 299 us; the launch traced here: 296 us
  starting transfers between devices  86.2 us (29%)
  waiting for transfers between devices  67.9 us (23%)
  local copies, waits for them, and re-layouts  62.3 us (21%)
  matrix products  47 us (16%)
  other arithmetic  24.6 us (8%)
  between operations  8.37 us (3%)
    ppermute x20, waiting for transfers between devices, shifted(): return lax.ppermute(value, 'seq', pairs)  62.4 us
    unnamed x101, local copies, waits for them, and re-layouts  47.2 us
    ppermute x20, starting transfers between devices, shifted(): return lax.ppermute(value, 'seq', pairs)  47.2 us
    dot_general x8, matrix products, exact(): return jnp.einsum(form, left, right, preferred_element_type=jnp.float32)  42.4 us
    ppermute x11, starting transfers between devices, swapped(): return lax.ppermute(value, 'seq', [(s, s ^ 1) for s in range(count)])  33.4 us
  transfers between devices with their start and end apart: 35, of which 11 were waited for; matrix products, arithmetic and copies ran while one was open for 27% of the time, Pallas kernels for 0%

profile of v3, /device:TPU:1, one launch (start us, length us, event | category | flops | bytes accessed | tf_op | source)
XLA Modules:
  0.0 296.4 jit_solution(16297654330988018593)
XLA Ops:
  7.6 8.7 %collective-permute-start.2 = (bf16[256,1152]{0,1:T(8,128)(2,1)}, bf16[256,1152]{0,1:T(8,128)(2,1)}, u32[]{:S(2)}, u32[]{:S(2)}) collective-permute-start(bf16[256,1152]{0,1:T(8,128)(2,1)} %get-tuple-element.222), channel_id=1, source_target_pairs={{0,8},{8,0},{16,24},{24,16},{32,40},{40,32},{48,56},{56,48},{64,72... | collective-permute-start | bytes 1769480 | tf_op jit(solution)/shard_map/ppermute | solution.py:37
  34.7 5.1 %collective-permute-done = f32[4,136,128]{2,1,0:T(8,128)S(1)} collective-permute-done((f32[4,136,128]{2,1,0:T(8,128)S(1)}, f32[4,136,128]{2,1,0:T(8,128)S(1)}, u32[]{:S(2)}, u32[]{:S(2)}) %collective-permute-start) | collective-permute-done | bytes 278560 | tf_op jit(solution)/shard_map/ppermute | solution.py:32
  47.4 5.2 %collective-permute-start.10 = (bf16[256,1152]{0,1:T(8,128)(2,1)S(1)}, bf16[256,1152]{0,1:T(8,128)(2,1)}, u32[]{:S(2)}, u32[]{:S(2)}) collective-permute-start(bf16[256,1152]{0,1:T(8,128)(2,1)S(1)} %collective-permute-done.4), channel_id=1, source_target_pairs={{0,16},{8,24},{16,32},{24,40},{32,48},{40,56},{48,64},{56,72},{64,... | collective-permute-start | bytes 1769480 | tf_op jit(solution)/shard_map/ppermute | solution.py:32
  63.7 11.3 %collective-permute-done.6 = f32[4,136,128]{2,1,0:T(8,128)S(1)} collective-permute-done((f32[4,136,128]{2,1,0:T(8,128)S(1)}, f32[4,136,128]{2,1,0:T(8,128)S(1)}, u32[]{:S(2)}, u32[]{:S(2)}) %collective-permute-start.6) | collective-permute-done | bytes 278560 | tf_op jit(solution)/shard_map/ppermute | solution.py:32
  83.9 4.0 %collective-permute-start.16 = (bf16[256,1152]{0,1:T(8,128)(2,1)}, bf16[256,1152]{0,1:T(8,128)(2,1)S(1)}, u32[]{:S(2)}, u32[]{:S(2)}) collective-permute-start(bf16[256,1152]{0,1:T(8,128)(2,1)} %collective-permute-done.10), channel_id=1, source_target_pairs={{0,16},{8,24},{16,32},{24,40},{32,48},{40,56},{48,64},{56,72},{64,... | collective-permute-start | bytes 1769480 | tf_op jit(solution)/shard_map/ppermute | solution.py:32
  102.6 12.3 %collective-permute-done.12 = f32[4,136,128]{2,1,0:T(8,128)S(1)} collective-permute-done((f32[4,136,128]{2,1,0:T(8,128)S(1)}, f32[4,136,128]{2,1,0:T(8,128)S(1)}, u32[]{:S(2)}, u32[]{:S(2)}) %collective-permute-start.12) | collective-permute-done | bytes 278560 | tf_op jit(solution)/shard_map/ppermute | solution.py:32
  114.9 4.6 %collective-permute-start.13 = (f32[4,136,128]{2,1,0:T(8,128)S(1)}, f32[4,136,128]{2,1,0:T(8,128)S(1)}, u32[]{:S(2)}, u32[]{:S(2)}) collective-permute-start(f32[4,136,128]{2,1,0:T(8,128)S(1)} %get-tuple-element.226), channel_id=1, source_target_pairs={{0,16},{8,24},{16,32},{24,40},{32,48},{40,56},{48,64},{56,72},{64,... | collective-permute-start | bytes 835592 | tf_op jit(solution)/shard_map/ppermute | solution.py:32
  124.6 3.6 %collective-permute-start.20 = (bf16[256,1152]{0,1:T(8,128)(2,1)S(1)}, bf16[256,1152]{0,1:T(8,128)(2,1)}, u32[]{:S(2)}, u32[]{:S(2)}) collective-permute-start(bf16[256,1152]{0,1:T(8,128)(2,1)S(1)} %collective-permute-done.16), channel_id=1, source_target_pairs={{0,8},{8,0},{16,24},{24,16},{32,40},{40,32},{48,56},{56,48},{64,72... | collective-permute-start | bytes 1769480 | tf_op jit(solution)/shard_map/ppermute | solution.py:37
  128.2 5.6 %collective-permute-start.22 = (bf16[256,1152]{0,1:T(8,128)(2,1)S(1)}, bf16[256,1152]{0,1:T(8,128)(2,1)}, u32[]{:S(2)}, u32[]{:S(2)}) collective-permute-start(bf16[256,1152]{0,1:T(8,128)(2,1)S(1)} %collective-permute-done.16), channel_id=1, source_target_pairs={{0,16},{8,24},{16,32},{24,40},{32,48},{40,56},{48,64},{56,72},{64,... | collective-permute-start | bytes 1769480 | tf_op jit(solution)/shard_map/ppermute | solution.py:32
  145.1 21.9 %collective-permute-done.18 = f32[4,136,128]{2,1,0:T(8,128)S(1)} collective-permute-done((f32[4,136,128]{2,1,0:T(8,128)S(1)}, f32[4,136,128]{2,1,0:T(8,128)S(1)}, u32[]{:S(2)}, u32[]{:S(2)}) %collective-permute-start.18) | collective-permute-done | bytes 278560 | tf_op jit(solution)/shard_map/ppermute | solution.py:32
  167.0 5.2 %collective-permute-start.19 = (f32[4,136,128]{2,1,0:T(8,128)S(1)}, f32[4,136,128]{2,1,0:T(8,128)S(1)}, u32[]{:S(2)}, u32[]{:S(2)}) collective-permute-start(f32[4,136,128]{2,1,0:T(8,128)S(1)} %get-tuple-element.224), channel_id=1, source_target_pairs={{0,32},{8,40},{16,48},{24,56},{32,64},{40,72},{48,80},{56,88},{64,... | collective-permute-start | bytes 835592 | tf_op jit(solution)/shard_map/ppermute | solution.py:32
  186.4 3.8 %collective-permute-start.24 = (bf16[256,1152]{0,1:T(8,128)(2,1)}, bf16[256,1152]{0,1:T(8,128)(2,1)S(1)}, u32[]{:S(2)}, u32[]{:S(2)}) collective-permute-start(bf16[256,1152]{0,1:T(8,128)(2,1)} %collective-permute-done.22), channel_id=1, source_target_pairs={{0,8},{8,0},{16,24},{24,16},{32,40},{40,32},{48,56},{56,48},{64,72... | collective-permute-start | bytes 1769480 | tf_op jit(solution)/shard_map/ppermute | solution.py:37
  205.4 2.9 fusion.101
  212.8 2.6 fusion.5
  215.4 4.6 %multiply_reduce_fusion = (f32[256,4]{0,1:T(4,128)S(1)}, bf16[256,4,128]{0,2,1:T(8,128)(2,1)}) fusion(bf16[256,512]{0,1:T(8,128)(2,1)S(1)} %copy.63, f32[256,4]{0,1:T(4,128)S(1)} %bitcast.259, bf16[2560,4,128]{0,2,1:T(8,128)(2,1)S(1)} %bitcast.247, f32[4,2560,256]{2,1,0:T(8,128)S(1)} %get-tuple-element.250, f32[4,256]{1,0:T(4,128)S(1)} %get-tuple-element.249, ...), kind=kOutput, calls=%fused_computation.63 | convolution fusion | flops 684981248 | bytes 14299136 | tf_op jit(solution)/shard_map/hts,shd->htd/dot_general | solution.py:15
  231.1 10.9 %fusion.31 = bf16[4,128,256]{2,1,0:T(8,128)(2,1)} fusion(bf16[2560,4,128]{0,2,1:T(8,128)(2,1)} %bitcast.238, f32[4,2560,256]{2,1,0:T(8,128)} %copy-done.2, bf16[2560,4,128]{0,2,1:T(8,128)(2,1)} %bitcast.248, bf16[256,4,128]{0,2,1:T(8,128)(2,1)} %bitcast.250, f32[4,256]{1,0:T(4,128)} %bitcast.262, f32[4,256]{1,0:T(4,128)} %copy-done.24, ...), kind=kOutput, calls=%fused_computation.44 | convolution fusion | flops 1360789504 | bytes 16916480 | tf_op jit(solution)/shard_map/hts,shd->thd/dot_general | solution.py:15
  242.0 4.5 %compare_and_fusion = pred[2560,256]{1,0:T(8,128)(4,1)} fusion(s32[256]{0:T(256)S(1)} %copy-done.23, s32[256]{0:T(256)} %iota_add_fusion.1, s32[2560]{0:T(1024)} %fusion.86, s32[2560]{0:T(1024)S(1)} %copy-done.21, pred[2560]{0:T(1024)(128)(4,1)} %broadcast_compare_fusion), kind=kLoop, calls=%fused_computation.21 | loop fusion | flops 2621440 | bytes 680448 | tf_op jit(solution)/shard_map/and | solution.py:202
  246.5 5.6 %fusion.51 = f32[4,2560,256]{2,1,0:T(8,128)} fusion(bf16[2560,4,128]{0,2,1:T(8,128)(2,1)S(1)} %bitcast.235, bf16[256,512]{1,0:T(8,128)(2,1)S(1)} %copy-done.7), kind=kOutput, calls=%fused_computation.71 | convolution fusion | flops 671088640 | bytes 13369344 | tf_op jit(solution)/shard_map/thd,shd->hts/dot_general | solution.py:15
  262.7 3.8 %collective-permute-done.31 = f32[2,4,256]{2,1,0:T(4,128)S(1)} collective-permute-done((f32[2,4,256]{2,1,0:T(4,128)}, f32[2,4,256]{2,1,0:T(4,128)S(1)}, u32[]{:S(2)}, u32[]{:S(2)}) %collective-permute-start.31) | collective-permute-done | bytes 8224 | tf_op jit(solution)/shard_map/ppermute | solution.py:32
  266.5 2.9 collective-permute-done.32
  269.5 4.1 %collective-permute-done.33 = f32[2,4,256]{2,1,0:T(4,128)S(1)} collective-permute-done((f32[2,4,256]{2,1,0:T(4,128)}, f32[2,4,256]{2,1,0:T(4,128)S(1)}, u32[]{:S(2)}, u32[]{:S(2)}) %collective-permute-start.33) | collective-permute-done | bytes 8224 | tf_op jit(solution)/shard_map/ppermute | solution.py:32
  273.6 2.6 collective-permute-done.34
  276.8 6.5 %fusion.32 = bf16[4,128,256]{2,1,0:T(8,128)(2,1)S(1)} fusion(bf16[2560,4,128]{0,2,1:T(8,128)(2,1)} %bitcast.245, f32[4,2560,256]{2,1,0:T(8,128)} %fusion.51, f32[4,2560]{1,0:T(4,128)S(1)} %get-tuple-element.220, pred[2560,256]{1,0:T(8,128)(4,1)} %compare_and_fusion), kind=kOutput, calls=%fused_computation.45 | convolution fusion | flops 684326912 | bytes 14065664 | tf_op jit(solution)/shard_map/hts,thd->shd/dot_general | solution.py:15
  283.4 10.4 %fusion.30 = bf16[4,128,256]{2,1,0:T(8,128)(2,1)} fusion(bf16[2560,4,128]{0,2,1:T(8,128)(2,1)S(1)} %bitcast.236, f32[4,2560,256]{2,1,0:T(8,128)} %fusion.51, f32[4,2560]{1,0:T(4,128)S(1)} %copy-done.22, f32[4,2560]{1,0:T(4,128)S(1)} %get-tuple-element.220, pred[2560,256]{1,0:T(8,128)(4,1)} %compare_and_fusion, bf16[2560,4,128]{0,2,1:T(8,128)(2,1)} %bitcast.246, ...), kind=kOutput, calls=%fused_computation.43 | convolution fusion | flops 1360789504 | bytes 16990208 | tf_op jit(solution)/shard_map/hts,thd->shd/dot_general | solution.py:15
  (239 shorter events, 135.5 us)
Async XLA Ops:
  7.6 37.9 %collective-permute-start.2 = (bf16[256,1152]{0,1:T(8,128)(2,1)}, bf16[256,1152]{0,1:T(8,128)(2,1)}, u32[]{:S(2)}, u32[]{:S(2)}) collective-permute-start(bf16[256,1152]{0,1:T(8,128)(2,1)} %get-tuple-element.222), channel_id=1, source_target_pairs={{0,8},{8,0},{16,24},{24,16},{32,40},{40,32},{48,56},{56,48},{64,72... | collective-permute-start | bytes 1769480 | tf_op jit(solution)/shard_map/ppermute | solution.py:37
  16.3 29.1 %collective-permute-start.4 = (bf16[256,1152]{0,1:T(8,128)(2,1)}, bf16[256,1152]{0,1:T(8,128)(2,1)S(1)}, u32[]{:S(2)}, u32[]{:S(2)}) collective-permute-start(bf16[256,1152]{0,1:T(8,128)(2,1)} %get-tuple-element.222), channel_id=1, source_target_pairs={{0,16},{8,24},{16,32},{24,40},{32,48},{40,56},{48,64},{56,72},{64,... | collective-permute-start | bytes 1769480 | tf_op jit(solution)/shard_map/ppermute | solution.py:32
  17.7 27.8 %collective-permute-start.3 = (bf16[256,1152]{0,1:T(8,128)(2,1)}, bf16[256,1152]{0,1:T(8,128)(2,1)}, u32[]{:S(2)}, u32[]{:S(2)}) collective-permute-start(bf16[256,1152]{0,1:T(8,128)(2,1)} %get-tuple-element.217), channel_id=1, source_target_pairs={{0,8},{8,0},{16,24},{24,16},{32,40},{40,32},{48,56},{56,48},{64,72... | collective-permute-start | bytes 1769480 | tf_op jit(solution)/shard_map/ppermute | solution.py:37
  19.6 25.9 %collective-permute-start.5 = (bf16[256,1152]{0,1:T(8,128)(2,1)}, bf16[256,1152]{0,1:T(8,128)(2,1)}, u32[]{:S(2)}, u32[]{:S(2)}) collective-permute-start(bf16[256,1152]{0,1:T(8,128)(2,1)} %get-tuple-element.217), channel_id=1, source_target_pairs={{16,0},{24,8},{32,16},{40,24},{48,32},{56,40},{64,48},{72,56},{80,... | collective-permute-start | bytes 1769480 | tf_op jit(solution)/shard_map/ppermute | solution.py:32
  45.5 35.3 %collective-permute-start.8 = (bf16[256,1152]{0,1:T(8,128)(2,1)S(1)}, bf16[256,1152]{0,1:T(8,128)(2,1)}, u32[]{:S(2)}, u32[]{:S(2)}) collective-permute-start(bf16[256,1152]{0,1:T(8,128)(2,1)S(1)} %collective-permute-done.4), channel_id=1, source_target_pairs={{0,8},{8,0},{16,24},{24,16},{32,40},{40,32},{48,56},{56,48},{64,72... | collective-permute-start | bytes 1769480 | tf_op jit(solution)/shard_map/ppermute | solution.py:37
  47.4 33.4 %collective-permute-start.10 = (bf16[256,1152]{0,1:T(8,128)(2,1)S(1)}, bf16[256,1152]{0,1:T(8,128)(2,1)}, u32[]{:S(2)}, u32[]{:S(2)}) collective-permute-start(bf16[256,1152]{0,1:T(8,128)(2,1)S(1)} %collective-permute-done.4), channel_id=1, source_target_pairs={{0,16},{8,24},{16,32},{24,40},{32,48},{40,56},{48,64},{56,72},{64,... | collective-permute-start | bytes 1769480 | tf_op jit(solution)/shard_map/ppermute | solution.py:32
  52.6 28.2 %collective-permute-start.9 = (bf16[256,1152]{0,1:T(8,128)(2,1)}, bf16[256,1152]{0,1:T(8,128)(2,1)}, u32[]{:S(2)}, u32[]{:S(2)}) collective-permute-start(bf16[256,1152]{0,1:T(8,128)(2,1)} %collective-permute-done.5), channel_id=1, source_target_pairs={{0,8},{8,0},{16,24},{24,16},{32,40},{40,32},{48,56},{56,48},{64,72... | collective-permute-start | bytes 1769480 | tf_op jit(solution)/shard_map/ppermute | solution.py:37
  54.8 26.0 %collective-permute-start.11 = (bf16[256,1152]{0,1:T(8,128)(2,1)}, bf16[256,1152]{0,1:T(8,128)(2,1)}, u32[]{:S(2)}, u32[]{:S(2)}) collective-permute-start(bf16[256,1152]{0,1:T(8,128)(2,1)} %collective-permute-done.5), channel_id=1, source_target_pairs={{16,0},{24,8},{32,16},{40,24},{48,32},{56,40},{64,48},{72,56},{80,... | collective-permute-start | bytes 1769480 | tf_op jit(solution)/shard_map/ppermute | solution.py:32
  81.5 43.1 %collective-permute-start.14 = (bf16[256,1152]{0,1:T(8,128)(2,1)}, bf16[256,1152]{0,1:T(8,128)(2,1)}, u32[]{:S(2)}, u32[]{:S(2)}) collective-permute-start(bf16[256,1152]{0,1:T(8,128)(2,1)} %collective-permute-done.10), channel_id=1, source_target_pairs={{0,8},{8,0},{16,24},{24,16},{32,40},{40,32},{48,56},{56,48},{64,72... | collective-permute-start | bytes 1769480 | tf_op jit(solution)/shard_map/ppermute | solution.py:37
  83.9 40.7 %collective-permute-start.16 = (bf16[256,1152]{0,1:T(8,128)(2,1)}, bf16[256,1152]{0,1:T(8,128)(2,1)S(1)}, u32[]{:S(2)}, u32[]{:S(2)}) collective-permute-start(bf16[256,1152]{0,1:T(8,128)(2,1)} %collective-permute-done.10), channel_id=1, source_target_pairs={{0,16},{8,24},{16,32},{24,40},{32,48},{40,56},{48,64},{56,72},{64,... | collective-permute-start | bytes 1769480 | tf_op jit(solution)/shard_map/ppermute | solution.py:32
  87.9 36.7 %collective-permute-start.15 = (bf16[256,1152]{0,1:T(8,128)(2,1)}, bf16[256,1152]{0,1:T(8,128)(2,1)}, u32[]{:S(2)}, u32[]{:S(2)}) collective-permute-start(bf16[256,1152]{0,1:T(8,128)(2,1)} %collective-permute-done.11), channel_id=1, source_target_pairs={{0,8},{8,0},{16,24},{24,16},{32,40},{40,32},{48,56},{56,48},{64,72... | collective-permute-start | bytes 1769480 | tf_op jit(solution)/shard_map/ppermute | solution.py:37
  90.1 34.5 %collective-permute-start.17 = (bf16[256,1152]{0,1:T(8,128)(2,1)}, bf16[256,1152]{0,1:T(8,128)(2,1)}, u32[]{:S(2)}, u32[]{:S(2)}) collective-permute-start(bf16[256,1152]{0,1:T(8,128)(2,1)} %collective-permute-done.11), channel_id=1, source_target_pairs={{16,0},{24,8},{32,16},{40,24},{48,32},{56,40},{64,48},{72,56},{80,... | collective-permute-start | bytes 1769480 | tf_op jit(solution)/shard_map/ppermute | solution.py:32
  97.3 17.5 %collective-permute-start.12 = (f32[4,136,128]{2,1,0:T(8,128)S(1)}, f32[4,136,128]{2,1,0:T(8,128)S(1)}, u32[]{:S(2)}, u32[]{:S(2)}) collective-permute-start(f32[4,136,128]{2,1,0:T(8,128)S(1)} %get-tuple-element.227), channel_id=1, source_target_pairs={{16,0},{24,8},{32,16},{40,24},{48,32},{56,40},{64,48},{72,56},{80,... | collective-permute-start | bytes 835592 | tf_op jit(solution)/shard_map/ppermute | solution.py:32
  124.6 52.6 %collective-permute-start.20 = (bf16[256,1152]{0,1:T(8,128)(2,1)S(1)}, bf16[256,1152]{0,1:T(8,128)(2,1)}, u32[]{:S(2)}, u32[]{:S(2)}) collective-permute-start(bf16[256,1152]{0,1:T(8,128)(2,1)S(1)} %collective-permute-done.16), channel_id=1, source_target_pairs={{0,8},{8,0},{16,24},{24,16},{32,40},{40,32},{48,56},{56,48},{64,72... | collective-permute-start | bytes 1769480 | tf_op jit(solution)/shard_map/ppermute | solution.py:37
  128.2 49.1 %collective-permute-start.22 = (bf16[256,1152]{0,1:T(8,128)(2,1)S(1)}, bf16[256,1152]{0,1:T(8,128)(2,1)}, u32[]{:S(2)}, u32[]{:S(2)}) collective-permute-start(bf16[256,1152]{0,1:T(8,128)(2,1)S(1)} %collective-permute-done.16), channel_id=1, source_target_pairs={{0,16},{8,24},{16,32},{24,40},{32,48},{40,56},{48,64},{56,72},{64,... | collective-permute-start | bytes 1769480 | tf_op jit(solution)/shard_map/ppermute | solution.py:32
  133.8 43.5 %collective-permute-start.21 = (bf16[256,1152]{0,1:T(8,128)(2,1)}, bf16[256,1152]{0,1:T(8,128)(2,1)}, u32[]{:S(2)}, u32[]{:S(2)}) collective-permute-start(bf16[256,1152]{0,1:T(8,128)(2,1)} %collective-permute-done.17), channel_id=1, source_target_pairs={{0,8},{8,0},{16,24},{24,16},{32,40},{40,32},{48,56},{56,48},{64,72... | collective-permute-start | bytes 1769480 | tf_op jit(solution)/shard_map/ppermute | solution.py:37
  136.0 41.3 %collective-permute-start.23 = (bf16[256,1152]{0,1:T(8,128)(2,1)}, bf16[256,1152]{0,1:T(8,128)(2,1)}, u32[]{:S(2)}, u32[]{:S(2)}) collective-permute-start(bf16[256,1152]{0,1:T(8,128)(2,1)} %collective-permute-done.17), channel_id=1, source_target_pairs={{16,0},{24,8},{32,16},{40,24},{48,32},{56,40},{64,48},{72,56},{80,... | collective-permute-start | bytes 1769480 | tf_op jit(solution)/shard_map/ppermute | solution.py:32
  140.9 26.1 %collective-permute-start.18 = (f32[4,136,128]{2,1,0:T(8,128)S(1)}, f32[4,136,128]{2,1,0:T(8,128)S(1)}, u32[]{:S(2)}, u32[]{:S(2)}) collective-permute-start(f32[4,136,128]{2,1,0:T(8,128)S(1)} %get-tuple-element.225), channel_id=1, source_target_pairs={{32,0},{40,8},{48,16},{56,24},{64,32},{72,40},{80,48},{88,56},{96,... | collective-permute-start | bytes 835592 | tf_op jit(solution)/shard_map/ppermute | solution.py:32
  186.4 17.1 %collective-permute-start.24 = (bf16[256,1152]{0,1:T(8,128)(2,1)}, bf16[256,1152]{0,1:T(8,128)(2,1)S(1)}, u32[]{:S(2)}, u32[]{:S(2)}) collective-permute-start(bf16[256,1152]{0,1:T(8,128)(2,1)} %collective-permute-done.22), channel_id=1, source_target_pairs={{0,8},{8,0},{16,24},{24,16},{32,40},{40,32},{48,56},{56,48},{64,72... | collective-permute-start | bytes 1769480 | tf_op jit(solution)/shard_map/ppermute | solution.py:37
  220.6 33.2 %collective-permute-start.26 = (f32[2,4,256]{2,1,0:T(4,128)}, f32[2,4,256]{2,1,0:T(4,128)}, u32[]{:S(2)}, u32[]{:S(2)}) collective-permute-start(f32[2,4,256]{2,1,0:T(4,128)} %get-tuple-element.232), channel_id=1, source_target_pairs={{0,8},{8,0},{16,24},{24,16},{32,40},{40,32},{48,56},{56,48},{64,72... | collective-permute-start | bytes 24584 | tf_op jit(solution)/shard_map/ppermute | solution.py:37
  223.0 32.8 %collective-permute-start.27 = (f32[2,4,256]{2,1,0:T(4,128)}, f32[2,4,256]{2,1,0:T(4,128)}, u32[]{:S(2)}, u32[]{:S(2)}) collective-permute-start(f32[2,4,256]{2,1,0:T(4,128)} %get-tuple-element.232), channel_id=1, source_target_pairs={{16,0},{24,8},{32,16},{40,24},{48,32},{56,40},{64,48},{72,56},{80,... | collective-permute-start | bytes 24584 | tf_op jit(solution)/shard_map/ppermute | solution.py:32
  224.3 33.5 %collective-permute-start.28 = (f32[2,4,256]{2,1,0:T(4,128)}, f32[2,4,256]{2,1,0:T(4,128)}, u32[]{:S(2)}, u32[]{:S(2)}) collective-permute-start(f32[2,4,256]{2,1,0:T(4,128)} %get-tuple-element.232), channel_id=1, source_target_pairs={{16,8},{24,0},{32,24},{40,16},{48,40},{56,32},{64,56},{72,48},{80,... | collective-permute-start | bytes 24584 | tf_op jit(solution)/shard_map/ppermute | solution.py:43
  225.6 34.2 %collective-permute-start.29 = (f32[2,4,256]{2,1,0:T(4,128)}, f32[2,4,256]{2,1,0:T(4,128)}, u32[]{:S(2)}, u32[]{:S(2)}) collective-permute-start(f32[2,4,256]{2,1,0:T(4,128)} %get-tuple-element.232), channel_id=1, source_target_pairs={{32,0},{40,8},{48,16},{56,24},{64,32},{72,40},{80,48},{88,56},{96,... | collective-permute-start | bytes 24584 | tf_op jit(solution)/shard_map/ppermute | solution.py:32
  226.9 35.1 %collective-permute-start.30 = (f32[2,4,256]{2,1,0:T(4,128)}, f32[2,4,256]{2,1,0:T(4,128)}, u32[]{:S(2)}, u32[]{:S(2)}) collective-permute-start(f32[2,4,256]{2,1,0:T(4,128)} %get-tuple-element.232), channel_id=1, source_target_pairs={{32,8},{40,0},{48,24},{56,16},{64,40},{72,32},{80,56},{88,48},{96,... | collective-permute-start | bytes 24584 | tf_op jit(solution)/shard_map/ppermute | solution.py:43
  (43 other events, 870.2 us)
